TPU v7x, 256 devices: a whole 4x4x8 slice. The times are simulated.
256 devices in a mesh: row: 64 (over z_hi, y, x), col: 4 (over z_lo, core).
Axes of the slice: x: 4, y: 4, z: 8 (z_hi: 4, z_lo: 2; z = z_hi * 2 + z_lo), core: 2. Of those that a mesh axis runs over, the one named last changes fastest.
Arguments:
- efield_x: float32 [256, 32, 512], P('row', 'col'), may hold values from -0.6 to 0.6
- efield_y: float32 [256, 32, 512], P('row', 'col'), may hold values from -0.6 to 0.6
- efield_z: float32 [256, 32, 512], P('row', 'col'), may hold values from -0.6 to 0.6
- hfield_x: float32 [256, 32, 512], P('row', 'col'), may hold values from -0.6 to 0.6
- hfield_y: float32 [256, 32, 512], P('row', 'col'), may hold values from -0.6 to 0.6
- hfield_z: float32 [256, 32, 512], P('row', 'col'), may hold values from -0.6 to 0.6
- permittivity: float32 [256, 32, 512], P('row', 'col'), may hold values from 1 to 4.4
- conductivity: float32 [256, 32, 512], P('row', 'col'), may hold values from 0.001 to 0.05
Outputs:
- next_ex: float32 [256, 32, 512], P('row', 'col')
- next_ey: float32 [256, 32, 512], P('row', 'col')
- next_ez: float32 [256, 32, 512], P('row', 'col')
- next_hx: float32 [256, 32, 512], P('row', 'col')
- next_hy: float32 [256, 32, 512], P('row', 'col')
- next_hz: float32 [256, 32, 512], P('row', 'col')
All inputs are finite; a program needn't handle non-finite values.
Results may differ from a plain program's by a relative error of at most 0.0055.
Values sent between devices are 32-bit elements; how exact they have to be, the bound alone decides.
No kernel may reach another device: no remote copies, remote signals or barrier semaphores. Data moves between devices by JAX's collectives and lax.ppermute only.
A program may use at most 64 MiB of HBM per device.

v0:
```python
import jax
import jax.numpy as jnp
from jax import lax
from jax.sharding import PartitionSpec as P

HALF_STEP = 30.0


def with_halo(cells, sides, width):
    for axis, dim in sides:
        count = lax.axis_size(axis)
        ends = count - 1
        head = lax.slice_in_dim(cells, 0, width, axis=dim)
        tail = lax.slice_in_dim(cells, cells.shape[dim] - width, cells.shape[dim], axis=dim)
        cells = jnp.concatenate(
            [
                lax.ppermute(tail, axis, [(i, (i + 1) % count) for i in range(ends)]),
                cells,
                lax.ppermute(head, axis, [((i + 1) % count, i) for i in range(ends)]),
            ],
            axis=dim,
        )
    return cells


def shifted(values, stride, line_axis, filler, forward):
    length = values.shape[line_axis]
    padding = jnp.full_like(lax.slice_in_dim(values, 0, stride, axis=line_axis), filler)
    if forward:
        return jnp.concatenate(
            [lax.slice_in_dim(values, stride, length, axis=line_axis), padding], line_axis
        )
    return jnp.concatenate(
        [padding, lax.slice_in_dim(values, 0, length - stride, axis=line_axis)], line_axis
    )


def diff_up(values, line_axis):
    return shifted(values, 1, line_axis, 0.0, True) - values


def diff_down(values, line_axis):
    return values - shifted(values, 1, line_axis, 0.0, False)


def reduce_lines(sub_diag, main_diag, super_diag, source, line_axis):
    length = source.shape[line_axis]
    stride = 1
    while stride < length:
        sub_lo = shifted(sub_diag, stride, line_axis, 0.0, False)
        mid_lo = shifted(main_diag, stride, line_axis, 1.0, False)
        sup_lo = shifted(super_diag, stride, line_axis, 0.0, False)
        src_lo = shifted(source, stride, line_axis, 0.0, False)
        sub_hi = shifted(sub_diag, stride, line_axis, 0.0, True)
        mid_hi = shifted(main_diag, stride, line_axis, 1.0, True)
        sup_hi = shifted(super_diag, stride, line_axis, 0.0, True)
        src_hi = shifted(source, stride, line_axis, 0.0, True)
        ratio_lo = sub_diag / mid_lo
        ratio_hi = super_diag / mid_hi
        sub_diag = -sub_lo * ratio_lo
        super_diag = -sup_hi * ratio_hi
        main_diag = main_diag - sup_lo * ratio_lo - sub_hi * ratio_hi
        source = source - src_lo * ratio_lo - src_hi * ratio_hi
        stride = stride * 2
    return source / main_diag


def line_flags(length, line_axis, rank):
    iota_shape = [1] * rank
    iota_shape[line_axis] = length
    where_line = lax.broadcasted_iota(jnp.int32, tuple(iota_shape), line_axis)
    return (where_line == 0, where_line == length - 1)


def line_system(coupling, is_first, is_final):
    sub_diag = jnp.where(is_first, 0.0, -coupling)
    main_diag = jnp.where(is_first, 1.0 + coupling, 1.0 + 2.0 * coupling)
    super_diag = jnp.where(is_final, 0.0, -coupling)
    return (sub_diag, main_diag, super_diag)


def solve_local(source, coupling, line_axis):
    is_first, is_final = line_flags(source.shape[line_axis], line_axis, source.ndim)
    sub_diag, main_diag, super_diag = line_system(coupling, is_first, is_final)
    return reduce_lines(sub_diag, main_diag, super_diag, source, line_axis)


def inside_mask(count_y, count_z):
    pos_y = (
        lax.axis_index("row") * count_y
        + lax.broadcasted_iota(jnp.int32, (count_y + 2, 1, 1), 0)
        - 1
    )
    pos_z = (
        lax.axis_index("col") * count_z
        + lax.broadcasted_iota(jnp.int32, (1, count_z + 2, 1), 1)
        - 1
    )
    inside = (
        (pos_y >= 0)
        & (pos_y < count_y * lax.axis_size("row"))
        & (pos_z >= 0)
        & (pos_z < count_z * lax.axis_size("col"))
    )
    return inside


class RowSystem:
    def __init__(self, coupling):
        count = coupling.shape[0]
        self.count = count
        row_index = lax.axis_index("row")
        is_first, is_final = line_flags(count, 0, 3)
        is_first = jnp.logical_and(is_first, row_index == 0)
        is_final = jnp.logical_and(is_final, row_index == lax.axis_size("row") - 1)
        sub, main, sup = line_system(coupling, is_first, is_final)
        self.sub, self.main, self.sup = sub, main, sup
        fwd_sub = [None] * count
        fwd_sup = [None] * count
        pivot = [None] * count
        pivot[1] = main[1]
        fwd_sub[1] = sub[1] / main[1]
        fwd_sup[1] = sup[1] / main[1]
        for level in range(2, count - 1):
            pivot[level] = main[level] - sub[level] * fwd_sup[level - 1]
            fwd_sub[level] = -sub[level] * fwd_sub[level - 1] / pivot[level]
            fwd_sup[level] = sup[level] / pivot[level]
        bwd_sub = [None] * count
        bwd_sup = [None] * count
        bwd_sub[count - 2] = fwd_sub[count - 2]
        bwd_sup[count - 2] = fwd_sup[count - 2]
        for level in range(count - 3, 0, -1):
            bwd_sub[level] = fwd_sub[level] - fwd_sup[level] * bwd_sub[level + 1]
            bwd_sup[level] = -fwd_sup[level] * bwd_sup[level + 1]
        last = count - 1
        self.pivot, self.fwd_sub, self.fwd_sup = pivot, fwd_sub, fwd_sup
        self.bwd_sub, self.bwd_sup = bwd_sub, bwd_sup
        self.head = [sub[0], main[0] - sup[0] * bwd_sub[1], -sup[0] * bwd_sup[1]]
        self.tail = [
            -sub[last] * fwd_sub[last - 1],
            main[last] - sub[last] * fwd_sup[last - 1],
            sup[last],
        ]

    def reduce_source(self, source):
        count = self.count
        sub = self.sub
        fwd_src = [None] * count
        fwd_src[1] = source[1] / self.pivot[1]
        for level in range(2, count - 1):
            fwd_src[level] = (source[level] - sub[level] * fwd_src[level - 1]) / self.pivot[level]
        bwd_src = [None] * count
        bwd_src[count - 2] = fwd_src[count - 2]
        for level in range(count - 3, 0, -1):
            bwd_src[level] = fwd_src[level] - self.fwd_sup[level] * bwd_src[level + 1]
        last = count - 1
        head_src = source[0] - self.sup[0] * bwd_src[1]
        tail_src = source[last] - sub[last] * fwd_src[last - 1]
        return bwd_src, head_src, tail_src

    def expand(self, bwd_src, first_vals, final_vals):
        rows = [first_vals]
        for level in range(1, self.count - 1):
            rows.append(
                bwd_src[level] - self.bwd_sub[level] * first_vals - self.bwd_sup[level] * final_vals
            )
        rows.append(final_vals)
        return rows


def to_solver(planes, parts):
    lead = planes.shape[:-2]
    count_z, count_x = planes.shape[-2:]
    per_z = parts // count_z
    width = count_x // per_z
    split = planes.reshape(lead + (count_z, per_z, width))
    rank = len(lead)
    order = (rank, rank + 1) + tuple(range(rank)) + (rank + 2,)
    split = jnp.transpose(split, order)
    return split.reshape((parts,) + lead + (width,))


def from_solver(chunks, count_z, count_x):
    parts, k, width = chunks.shape
    per_z = parts // count_z
    split = chunks.reshape((count_z, per_z, k, width))
    split = jnp.transpose(split, (2, 0, 1, 3))
    return split.reshape((k, count_z, count_x))


def reduced_solve(matrix, rhs, want_prev):
    solved = reduce_lines(matrix[0], matrix[1], matrix[2], rhs, 0)
    parts = solved.shape[0] // 2
    pairs = solved.reshape((parts, 2) + solved.shape[1:])
    heads = pairs[:, 0]
    tails = pairs[:, 1]
    zero = jnp.zeros_like(heads[:1])
    next_heads = jnp.concatenate([heads[1:], zero], 0)
    outs = [heads, tails, next_heads]
    if want_prev:
        outs.append(jnp.concatenate([zero, tails[:-1]], 0))
    return jnp.stack(outs, 1)


def on_device(
    efield_x, efield_y, efield_z, hfield_x, hfield_y, hfield_z, permittivity, conductivity
):
    count_y = efield_x.shape[0]
    count_z = efield_x.shape[1]
    count_x = efield_x.shape[2]
    rows = lax.axis_size("row")
    col_index = lax.axis_index("col")

    ext = with_halo(
        jnp.stack(
            [efield_x, efield_y, efield_z, hfield_x, hfield_y, hfield_z, permittivity, conductivity]
        ),
        (("row", 1), ("col", 2)),
        1,
    )
    inside = inside_mask(count_y, count_z)
    ex_e, ey_e, ez_e = ext[0], ext[1], ext[2]
    hx_e, hy_e, hz_e = ext[3], ext[4], ext[5]
    eps_e = jnp.where(inside, ext[6], 1.0)
    sig_e = jnp.where(inside, ext[7], 0.0)
    damping = sig_e * HALF_STEP / (2.0 * eps_e)
    keep_e = (1.0 - damping) / (1.0 + damping)
    drive_e = HALF_STEP / (eps_e * (1.0 + damping))
    coup_e = drive_e * HALF_STEP

    ys = slice(1, count_y + 1)
    zs = slice(1, count_z + 1)
    keep = keep_e[ys, zs]
    drive = drive_e[ys, zs]
    coupling = coup_e[ys, zs]

    dpx_ey = diff_up(ey_e[0 : count_y + 1, zs], 2)
    source_x = keep * efield_x + drive * (
        (hz_e[ys, zs] - hz_e[0:count_y, zs])
        - (hy_e[ys, zs] - hy_e[ys, 0:count_z])
        - HALF_STEP * (dpx_ey[1:] - dpx_ey[:-1])
    )
    ya = slice(0, count_y + 1)
    dpy_ez = ez_e[1 : count_y + 2, 0 : count_z + 1] - ez_e[0 : count_y + 1, 0 : count_z + 1]
    source_y = keep_e[ya, zs] * ey_e[ya, zs] + drive_e[ya, zs] * (
        (hx_e[ya, zs] - hx_e[ya, 0:count_z])
        - diff_down(hz_e[ya, zs], 2)
        - HALF_STEP * (dpy_ez[:, 1:] - dpy_ez[:, :-1])
    )
    za = slice(0, count_z + 1)
    dpz_ex = ex_e[ys, 1 : count_z + 2] - ex_e[ys, 0 : count_z + 1]
    source_z = keep_e[ys, za] * ez_e[ys, za] + drive_e[ys, za] * (
        diff_down(hy_e[ys, za], 2)
        - (hx_e[ys, za] - hx_e[0:count_y, za])
        - HALF_STEP * diff_down(dpz_ex, 2)
    )

    gathered = lax.all_gather(
        jnp.stack([source_y, coup_e[ya, zs]]), "col", axis=2, tiled=True
    )
    coup_full = gathered[1]
    half_ey_full = solve_local(gathered[0], coup_full, 1)
    pos_y = (
        lax.axis_index("row") * count_y
        + lax.broadcasted_iota(jnp.int32, (count_y + 1, 1, 1), 0)
        - 1
    )
    half_ey_full = jnp.where(pos_y >= 0, half_ey_full, 0.0)
    padded = jnp.pad(half_ey_full, ((0, 0), (1, 1), (0, 0)))
    half_ey_e = lax.dynamic_slice_in_dim(padded, col_index * count_z, count_z + 2, axis=1)

    half_ez_e = solve_local(source_z, coup_e[ys, za], 2)
    half_ez_e = jnp.where(inside[ys, za], half_ez_e, 0.0)

    system = RowSystem(coupling)
    bwd_src, head_src, tail_src = system.reduce_source(source_x)
    parts = rows
    payload = jnp.stack(
        [
            jnp.stack(system.head + [head_src]),
            jnp.stack(system.tail + [tail_src]),
        ],
        1,
    )
    payload = to_solver(payload, parts)
    received = lax.all_to_all(payload, "row", split_axis=0, concat_axis=0, tiled=True)
    width = received.shape[-1]
    received = jnp.transpose(received, (1, 0, 2, 3)).reshape((4, parts * 2, width))
    matrix = received[:3]
    answer = reduced_solve(matrix, received[3], True)
    back = lax.all_to_all(answer, "row", split_axis=0, concat_axis=0, tiled=True)
    bounds = from_solver(back, count_z, count_x)
    half_ex_rows = system.expand(bwd_src, bounds[0], bounds[1])
    half_ex_e = jnp.stack([bounds[3]] + half_ex_rows + [bounds[2]])

    inside_e = inside
    half_hz_e = hz_e[ya, zs] + HALF_STEP * (
        (half_ex_e[1:] - half_ex_e[:-1]) - diff_up(ey_e[ya, zs], 2)
    )
    half_hz_e = jnp.where(inside_e[ya, zs], half_hz_e, 0.0)
    half_hy_e = hy_e[ys, za] + HALF_STEP * (diff_up(half_ez_e, 2) - dpz_ex)
    half_hy_e = jnp.where(inside_e[ys, za], half_hy_e, 0.0)
    dz_half_ey = half_ey_e[:, 1:] - half_ey_e[:, :-1]
    half_hx_e = hx_e[ya, za] + HALF_STEP * (dz_half_ey[:, 0 : count_z + 1] - dpy_ez)
    half_hx_e = jnp.where(inside_e[ya, za], half_hx_e, 0.0)

    half_ex = half_ex_e[1 : count_y + 1]
    half_ey = half_ey_e[1 : count_y + 1, 1 : count_z + 1]
    half_ez = half_ez_e[:, 1:]
    dx_half_ez = diff_up(half_ez_e, 2)
    dy_half_ex = half_ex_e[2:] - half_ex_e[1:-1]
    second_x = keep * half_ex + drive * (
        (half_hz_e[1:] - half_hz_e[:-1])
        - (half_hy_e[:, 1:] - half_hy_e[:, :-1])
        - HALF_STEP * (dx_half_ez[:, 1:] - dx_half_ez[:, :-1])
    )
    second_y = keep * half_ey + drive * (
        (half_hx_e[1:, 1:] - half_hx_e[1:, :-1])
        - diff_down(half_hz_e[1:], 2)
        - HALF_STEP * diff_down(dy_half_ex, 2)
    )
    dz_ey_own = dz_half_ey[:, 1 : count_z + 1]
    second_z = keep * half_ez + drive * (
        diff_down(half_hy_e[:, 1:], 2)
        - (half_hx_e[1:, 1:] - half_hx_e[:-1, 1:])
        - HALF_STEP * (dz_ey_own[1:] - dz_ey_own[:-1])
    )

    second_full = lax.all_gather(second_x, "col", axis=1, tiled=True)
    next_ex_full = solve_local(second_full, coup_full[1:], 1)
    padded = jnp.pad(next_ex_full, ((0, 0), (0, 1), (0, 0)))
    next_ex_e = lax.dynamic_slice_in_dim(padded, col_index * count_z, count_z + 1, axis=1)
    next_ex = next_ex_e[:, :-1]

    next_ey = solve_local(second_y, coupling, 2)

    bwd_src, head_src, tail_src = system.reduce_source(second_z)
    payload = to_solver(jnp.stack([head_src, tail_src]), parts)
    received = lax.all_to_all(payload, "row", split_axis=0, concat_axis=0, tiled=True)
    answer = reduced_solve(matrix, received.reshape((parts * 2, width)), False)
    back = lax.all_to_all(answer, "row", split_axis=0, concat_axis=0, tiled=True)
    bounds = from_solver(back, count_z, count_x)
    next_ez_rows = system.expand(bwd_src, bounds[0], bounds[1])
    next_ez = jnp.stack(next_ez_rows)
    next_ez_e = jnp.stack(next_ez_rows + [bounds[2]])

    next_hx = half_hx_e[1:, 1:] + HALF_STEP * (
        dz_ey_own[1:] - (next_ez_e[1:] - next_ez_e[:-1])
    )
    next_hy = half_hy_e[:, 1:] + HALF_STEP * (
        dx_half_ez[:, 1:] - (next_ex_e[:, 1:] - next_ex_e[:, :-1])
    )
    next_hz = half_hz_e[1:] + HALF_STEP * (dy_half_ex - diff_up(next_ey, 2))
    return (next_ex, next_ey, next_ez, next_hx, next_hy, next_hz)


def solution(mesh):
    spec = P("row", "col", None)
    return jax.shard_map(
        on_device,
        mesh=mesh,
        in_specs=(spec,) * 8,
        out_specs=(spec,) * 6,
        check_vma=False,
    )
```

profile of v0, /device:TPU:1, one launch (start us, length us, event | category | flops | bytes accessed | tf_op | source)
XLA Modules:
  0.0 157.2 jit_solution(13735154062393251268)
XLA Ops:
  0.6 0.8 bitcast_dynamic-update-slice_fusion.7
  1.5 0.8 bitcast_dynamic-update-slice_fusion.6
  2.3 0.8 bitcast_dynamic-update-slice_fusion.5
  3.2 0.8 bitcast_dynamic-update-slice_fusion.4
  7.4 1.3 collective-permute-start.1
  8.7 4.6 %collective-permute-start = (f32[8,1,8,512]{3,2,1,0:T(8,128)S(1)}, f32[8,1,8,512]{3,2,1,0:T(8,128)S(1)}, u32[]{:S(2)}, u32[]{:S(2)}) collective-permute-start(f32[8,1,8,512]{3,2,1,0:T(8,128)S(1)} %get-tuple-element.150), channel_id=1, source_target_pairs={{0,4},{4,8},{8,12},{12,16},{16,20},{20,24},{24,28},{28,32},{32,36}... | collective-permute-start | bytes 393224 | tf_op jit(solution)/shard_map/ppermute | solution.py:17
  14.2 1.0 collective-permute-done
  15.3 5.7 %collective-permute-start.3 = (f32[8,6,1,512]{3,2,1,0:T(1,128)S(1)}, f32[8,6,1,512]{3,2,1,0:T(1,128)S(1)}, u32[]{:S(2)}, u32[]{:S(2)}) collective-permute-start(f32[8,6,1,512]{3,2,1,0:T(1,128)S(1)} %get-tuple-element.146), channel_id=1, source_target_pairs={{1,0},{2,1},{3,2},{5,4},{6,5},{7,6},{9,8},{10,9},{11,10},{13,12},{... | collective-permute-start | bytes 294920 | tf_op jit(solution)/shard_map/ppermute | solution.py:19
  21.0 1.9 %collective-permute-start.2 = (f32[8,6,1,512]{3,2,1,0:T(1,128)S(1)}, f32[8,6,1,512]{3,2,1,0:T(1,128)S(1)}, u32[]{:S(2)}, u32[]{:S(2)}) collective-permute-start(f32[8,6,1,512]{3,2,1,0:T(1,128)S(1)} %get-tuple-element.145), channel_id=1, source_target_pairs={{0,1},{1,2},{2,3},{4,5},{5,6},{6,7},{8,9},{9,10},{10,11},{12,13},{... | collective-permute-start | bytes 294920 | tf_op jit(solution)/shard_map/ppermute | solution.py:17
  23.0 1.5 collective-permute-done.3
  25.4 9.0 %all_gather.7 = f32[2,5,32,512]{3,2,1,0:T(8,128)S(1)} all-gather(f32[2,5,8,512]{3,2,1,0:T(8,128)S(1)} %pad_maximum_fusion.2), channel_id=1, replica_groups=mesh['row'=64,'col'=4] {'col'}, dimensions={2}, use_global_device_ids=true | all-gather | bytes 819200 | tf_op jit(solution)/shard_map/all_gather | solution.py:258
  48.1 21.9 %all-to-all-start.2 = ((f32[64,1,128]{2,1,0:T(1,128)}), f32[64,1,128]{2,1,0:T(1,128)S(1)}, u32[]{:S(2)}, u32[]{:S(2)}) async-start(f32[64,1,128]{2,1,0:T(1,128)} %reshape.289), calls=%async_computation.2 | async-start | bytes 65536 | tf_op jit(solution)/shard_map/all_to_all | solution.py:339
  70.8 0.9 reshape.285
  71.8 8.7 %all-to-all-done.2 = f32[64,1,128]{2,1,0:T(1,128)S(1)} async-done(((f32[64,1,128]{2,1,0:T(1,128)}), f32[64,1,128]{2,1,0:T(1,128)S(1)}, u32[]{:S(2)}, u32[]{:S(2)}) %all-to-all-start.2) | async-done | bytes 32800 | tf_op jit(solution)/shard_map/all_to_all | solution.py:339
  80.5 4.6 %all-to-all-start = ((f32[64,1,512]{2,1,0:T(1,128)}), f32[64,1,512]{2,1,0:T(1,128)S(1)}, u32[]{:S(2)}, u32[]{:S(2)}) async-start(f32[64,1,512]{2,1,0:T(1,128)} %reshape.285), calls=%async_computation | async-start | bytes 262144 | tf_op jit(solution)/shard_map/all_to_all | solution.py:286
  87.3 9.1 %all-to-all-done = f32[64,1,512]{2,1,0:T(1,128)S(1)} async-done(((f32[64,1,512]{2,1,0:T(1,128)}), f32[64,1,512]{2,1,0:T(1,128)S(1)}, u32[]{:S(2)}, u32[]{:S(2)}) %all-to-all-start) | async-done | bytes 131104 | tf_op jit(solution)/shard_map/all_to_all | solution.py:286
  96.4 1.0 reduce.29
  97.7 0.9 multiply_subtract_fusion.37
  101.0 4.6 %all-to-all-start.3 = ((f32[64,1,192]{2,1,0:T(1,128)}), f32[64,1,192]{2,1,0:T(1,128)S(1)}, u32[]{:S(2)}, u32[]{:S(2)}) async-start(f32[64,1,192]{2,1,0:T(1,128)} %reshape.291), calls=%async_computation.3 | async-start | bytes 131072 | tf_op jit(solution)/shard_map/all_to_all | solution.py:341
  106.5 10.0 %all-to-all-done.3 = f32[64,1,192]{2,1,0:T(1,128)S(1)} async-done(((f32[64,1,192]{2,1,0:T(1,128)}), f32[64,1,192]{2,1,0:T(1,128)S(1)}, u32[]{:S(2)}, u32[]{:S(2)}) %all-to-all-start.3) | async-done | bytes 49184 | tf_op jit(solution)/shard_map/all_to_all | solution.py:341
  116.5 4.7 %all-to-all-start.1 = ((f32[64,1,256]{2,1,0:T(1,128)}), f32[64,1,256]{2,1,0:T(1,128)S(1)}, u32[]{:S(2)}, u32[]{:S(2)}) async-start(f32[64,1,256]{2,1,0:T(1,128)} %reshape.287), calls=%async_computation.1 | async-start | bytes 131072 | tf_op jit(solution)/shard_map/all_to_all | solution.py:291
  123.2 8.8 %all-to-all-done.1 = f32[64,1,256]{2,1,0:T(1,128)S(1)} async-done(((f32[64,1,256]{2,1,0:T(1,128)}), f32[64,1,256]{2,1,0:T(1,128)S(1)}, u32[]{:S(2)}, u32[]{:S(2)}) %all-to-all-start.1) | async-done | bytes 65568 | tf_op jit(solution)/shard_map/all_to_all | solution.py:291
  140.7 11.0 %all_gather.6 = f32[4,32,512]{2,1,0:T(8,128)S(1)} all-gather(f32[4,8,512]{2,1,0:T(8,128)S(1)} %get-tuple-element.329), channel_id=1, replica_groups=mesh['row'=64,'col'=4] {'col'}, dimensions={1}, use_global_device_ids=true | all-gather | bytes 327680 | tf_op jit(solution)/shard_map/all_gather | solution.py:329
  155.6 1.6 %fusion.44 = (f32[4,8,512]{2,1,0:T(8,128)}, f32[4,8,512]{2,1,0:T(8,128)}) fusion(f32[1,8,512]{2,1,0:T(8,128)S(1)} %copy-done.11, f32[1,8,512]{2,1,0:T(8,128)S(1)} %squeeze.44, f32[1,8,512]{2,1,0:T(8,128)S(1)} %get-tuple-element.473, f32[1,8,512]{2,1,0:T(8,128)S(1)} %get-tuple-element.324, f32[5,9,512]{2,1,0:T(8,128)} %copy-done, ...), kind=kLoop, calls=%fused_computation.208 | loop fusion | flops 163840 | bytes 344064 | tf_op jit(solution)/shard_map/add | solution.py:347
  (353 shorter events, 38.3 us)
Async XLA Ops:
  7.4 6.8 %collective-permute-start.1 = (f32[8,1,8,512]{3,2,1,0:T(8,128)S(1)}, f32[8,1,8,512]{3,2,1,0:T(8,128)S(1)}, u32[]{:S(2)}, u32[]{:S(2)}) collective-permute-start(f32[8,1,8,512]{3,2,1,0:T(8,128)S(1)} %get-tuple-element.151), channel_id=1, source_target_pairs={{4,0},{8,4},{12,8},{16,12},{20,16},{24,20},{28,24},{32,28},{36,32}... | collective-permute-start | bytes 393224 | tf_op jit(solution)/shard_map/ppermute | solution.py:19
  8.7 6.5 %collective-permute-start = (f32[8,1,8,512]{3,2,1,0:T(8,128)S(1)}, f32[8,1,8,512]{3,2,1,0:T(8,128)S(1)}, u32[]{:S(2)}, u32[]{:S(2)}) collective-permute-start(f32[8,1,8,512]{3,2,1,0:T(8,128)S(1)} %get-tuple-element.150), channel_id=1, source_target_pairs={{0,4},{4,8},{8,12},{12,16},{16,20},{20,24},{24,28},{28,32},{32,36}... | collective-permute-start | bytes 393224 | tf_op jit(solution)/shard_map/ppermute | solution.py:17
  13.3 21.5 %copy-start.18 = (pred[32]{0:T(512)(128)(4,1)}, pred[32]{0:T(512)(128)(4,1)S(1)}, u32[]{:S(2)}) copy-start(pred[32]{0:T(512)(128)(4,1)S(1)} %get-tuple-element.481) | copy-start | bytes 100
  13.3 22.0 %copy-start.12 = (pred[32]{0:T(512)(128)(4,1)}, pred[32]{0:T(512)(128)(4,1)S(1)}, u32[]{:S(2)}) copy-start(pred[32]{0:T(512)(128)(4,1)S(1)} %get-tuple-element.482) | copy-start | bytes 100
  14.2 24.8 %copy-start.16 = (pred[512]{0:T(512)(128)(4,1)}, pred[512]{0:T(512)(128)(4,1)S(1)}, u32[]{:S(2)}) copy-start(pred[512]{0:T(512)(128)(4,1)S(1)} %get-tuple-element.483) | copy-start | bytes 1540
  14.2 30.6 %copy-start.14 = (pred[512]{0:T(512)(128)(4,1)}, pred[512]{0:T(512)(128)(4,1)S(1)}, u32[]{:S(2)}) copy-start(pred[512]{0:T(512)(128)(4,1)S(1)} %get-tuple-element.484) | copy-start | bytes 1540
  15.3 9.1 %collective-permute-start.3 = (f32[8,6,1,512]{3,2,1,0:T(1,128)S(1)}, f32[8,6,1,512]{3,2,1,0:T(1,128)S(1)}, u32[]{:S(2)}, u32[]{:S(2)}) collective-permute-start(f32[8,6,1,512]{3,2,1,0:T(1,128)S(1)} %get-tuple-element.146), channel_id=1, source_target_pairs={{1,0},{2,1},{3,2},{5,4},{6,5},{7,6},{9,8},{10,9},{11,10},{13,12},{... | collective-permute-start | bytes 294920 | tf_op jit(solution)/shard_map/ppermute | solution.py:19
  21.0 3.5 %collective-permute-start.2 = (f32[8,6,1,512]{3,2,1,0:T(1,128)S(1)}, f32[8,6,1,512]{3,2,1,0:T(1,128)S(1)}, u32[]{:S(2)}, u32[]{:S(2)}) collective-permute-start(f32[8,6,1,512]{3,2,1,0:T(1,128)S(1)} %get-tuple-element.145), channel_id=1, source_target_pairs={{0,1},{1,2},{2,3},{4,5},{5,6},{6,7},{8,9},{9,10},{10,11},{12,13},{... | collective-permute-start | bytes 294920 | tf_op jit(solution)/shard_map/ppermute | solution.py:17
  45.3 24.9 %copy-start = (f32[5,9,512]{2,1,0:T(8,128)}, f32[5,9,512]{2,1,0:T(8,128)S(1)}, u32[]{:S(2)}) copy-start(f32[5,9,512]{2,1,0:T(8,128)S(1)} %get-tuple-element.74) | copy-start | bytes 276484
  45.9 24.1 %copy-start.3 = (f32[4,8,512]{2,1,0:T(8,128)}, f32[4,8,512]{2,1,0:T(8,128)S(1)}, u32[]{:S(2)}) copy-start(f32[4,8,512]{2,1,0:T(8,128)S(1)} %get-tuple-element.156) | copy-start | bytes 196612
  45.9 24.5 %copy-start.2 = (f32[4,8,512]{2,1,0:T(8,128)}, f32[4,8,512]{2,1,0:T(8,128)S(1)}, u32[]{:S(2)}) copy-start(f32[4,8,512]{2,1,0:T(8,128)S(1)} %get-tuple-element.155) | copy-start | bytes 196612
  48.1 32.4 %all-to-all-start.2 = ((f32[64,1,128]{2,1,0:T(1,128)}), f32[64,1,128]{2,1,0:T(1,128)S(1)}, u32[]{:S(2)}, u32[]{:S(2)}) async-start(f32[64,1,128]{2,1,0:T(1,128)} %reshape.289), calls=%async_computation.2 | async-start | bytes 65536 | tf_op jit(solution)/shard_map/all_to_all | solution.py:339
  80.5 15.9 %all-to-all-start = ((f32[64,1,512]{2,1,0:T(1,128)}), f32[64,1,512]{2,1,0:T(1,128)S(1)}, u32[]{:S(2)}, u32[]{:S(2)}) async-start(f32[64,1,512]{2,1,0:T(1,128)} %reshape.285), calls=%async_computation | async-start | bytes 262144 | tf_op jit(solution)/shard_map/all_to_all | solution.py:286
  100.0 33.7 %copy-start.6 = (f32[1,8,512]{2,1,0:T(8,128)S(1)}, f32[1,8,512]{2,1,0:T(8,128)}, u32[]{:S(2)}) copy-start(f32[1,8,512]{2,1,0:T(8,128)} %copy-done.5) | copy-start | bytes 49156
  100.0 33.7 %copy-start.8 = (f32[1,8,512]{2,1,0:T(8,128)S(1)}, f32[1,8,512]{2,1,0:T(8,128)}, u32[]{:S(2)}) copy-start(f32[1,8,512]{2,1,0:T(8,128)} %copy-done.7) | copy-start | bytes 49156
  100.1 34.4 %copy-start.10 = (f32[1,8,512]{2,1,0:T(8,128)S(1)}, f32[1,8,512]{2,1,0:T(8,128)}, u32[]{:S(2)}) copy-start(f32[1,8,512]{2,1,0:T(8,128)} %copy-done.9) | copy-start | bytes 49156
  101.0 15.5 %all-to-all-start.3 = ((f32[64,1,192]{2,1,0:T(1,128)}), f32[64,1,192]{2,1,0:T(1,128)S(1)}, u32[]{:S(2)}, u32[]{:S(2)}) async-start(f32[64,1,192]{2,1,0:T(1,128)} %reshape.291), calls=%async_computation.3 | async-start | bytes 131072 | tf_op jit(solution)/shard_map/all_to_all | solution.py:341
  116.5 15.6 %all-to-all-start.1 = ((f32[64,1,256]{2,1,0:T(1,128)}), f32[64,1,256]{2,1,0:T(1,128)S(1)}, u32[]{:S(2)}, u32[]{:S(2)}) async-start(f32[64,1,256]{2,1,0:T(1,128)} %reshape.287), calls=%async_computation.1 | async-start | bytes 131072 | tf_op jit(solution)/shard_map/all_to_all | solution.py:291
  132.9 2.6 %copy-start.15 = (pred[512]{0:T(512)(128)(4,1)S(1)}, pred[512]{0:T(512)(128)(4,1)}, u32[]{:S(2)}) copy-start(pred[512]{0:T(512)(128)(4,1)} %copy-done.14) | copy-start | bytes 1540
  132.9 2.6 %copy-start.17 = (pred[512]{0:T(512)(128)(4,1)S(1)}, pred[512]{0:T(512)(128)(4,1)}, u32[]{:S(2)}) copy-start(pred[512]{0:T(512)(128)(4,1)} %copy-done.16) | copy-start | bytes 1540
  139.8 12.0 %copy-start.13 = (pred[32]{0:T(512)(128)(4,1)S(1)}, pred[32]{0:T(512)(128)(4,1)}, u32[]{:S(2)}) copy-start(pred[32]{0:T(512)(128)(4,1)} %copy-done.12) | copy-start | bytes 100
  139.8 12.0 %copy-start.19 = (pred[32]{0:T(512)(128)(4,1)S(1)}, pred[32]{0:T(512)(128)(4,1)}, u32[]{:S(2)}) copy-start(pred[32]{0:T(512)(128)(4,1)} %copy-done.18) | copy-start | bytes 100
  139.9 12.1 %copy-start.1 = (f32[4,8,512]{2,1,0:T(8,128)}, f32[4,8,512]{2,1,0:T(8,128)S(1)}, u32[]{:S(2)}) copy-start(f32[4,8,512]{2,1,0:T(8,128)S(1)} %subtract_divide_fusion.3) | copy-start | bytes 196612
  154.6 1.0 copy-start.11
  (4 other events, 2.9 us)
where the time goes:
time: 158 us; the launch traced here: 157 us
  starting transfers between devices  49.3 us (31%)
  waiting for transfers between devices  39.1 us (25%)
  local copies, waits for them, and re-layouts  23.4 us (15%)
  other arithmetic  22.5 us (14%)
  blocking collectives  20 us (13%)
  between operations  2.75 us (2%)
    all_to_all x2, starting transfers between devices, on_device(): lax.all_to_all(payload, 'row', split_axis=0, concat_axis=0, tiled=True)  26.5 us
    all_to_all x2, waiting for transfers between devices, on_device(): lax.all_to_all(answer, 'row', split_axis=0, concat_axis=0, tiled=True)  18.7 us
    all_to_all x2, waiting for transfers between devices, on_device(): lax.all_to_all(payload, 'row', split_axis=0, concat_axis=0, tiled=True)  17.8 us
    all_gather x1, blocking collectives, on_device(): second_full = lax.all_gather(second_x, 'col', axis=1, tiled=True)  11 us
    unnamed x62, local copies, waits for them, and re-layouts  10.7 us
    all_to_all x2, starting transfers between devices, on_device(): lax.all_to_all(answer, 'row', split_axis=0, concat_axis=0, tiled=True)  9.31 us
    all_gather x1, blocking collectives, on_device(): lax.all_gather(jnp.stack([source_y, coup_e[ya, zs]]), 'col', axis=2, tile...  9.03 us
    ppermute x2, starting transfers between devices, with_halo(): lax.ppermute(head, axis, [((i + 1) % count, i) for i in range(ends)])  6.96 us
  transfers between devices with their start and end apart: 8, of which 7 were waited for; matrix products, arithmetic and copies ran while one was open for 5% of the time, Pallas kernels for 0%

commit v1 on v0

--- a/solution.py
+++ b/solution.py
@@ -189,17 +189,39 @@
 
 
 def reduced_solve(matrix, rhs, want_prev):
-    solved = reduce_lines(matrix[0], matrix[1], matrix[2], rhs, 0)
-    parts = solved.shape[0] // 2
-    pairs = solved.reshape((parts, 2) + solved.shape[1:])
-    heads = pairs[:, 0]
-    tails = pairs[:, 1]
-    zero = jnp.zeros_like(heads[:1])
-    next_heads = jnp.concatenate([heads[1:], zero], 0)
-    outs = [heads, tails, next_heads]
-    if want_prev:
-        outs.append(jnp.concatenate([zero, tails[:-1]], 0))
+    solved = reduce_lines(matrix[0][None], matrix[1][None], matrix[2][None], rhs, 1)
+    parts = solved.shape[1] // 2
+    outs = []
+    for one in range(solved.shape[0]):
+        pairs = solved[one].reshape((parts, 2) + solved.shape[2:])
+        heads = pairs[:, 0]
+        tails = pairs[:, 1]
+        zero = jnp.zeros_like(heads[:1])
+        outs += [heads, tails]
+    for one in range(solved.shape[0]):
+        heads = outs[2 * one]
+        outs.append(jnp.concatenate([heads[1:], zero], 0))
+    outs.append(jnp.concatenate([zero, outs[1][:-1]], 0))
     return jnp.stack(outs, 1)
+
+
+def field_halos(fields):
+    rows = lax.axis_size("row")
+    cols = lax.axis_size("col")
+    down_rows = [(i, i + 1) for i in range(rows - 1)]
+    up_rows = [(i + 1, i) for i in range(rows - 1)]
+    down_cols = [(i, i + 1) for i in range(cols - 1)]
+    up_cols = [(i + 1, i) for i in range(cols - 1)]
+    from_prev = lax.ppermute(jnp.stack([f[-1:] for f in fields]), "row", down_rows)
+    from_next = lax.ppermute(jnp.stack([f[:1] for f in fields]), "row", up_rows)
+    ext_y = [
+        jnp.concatenate([from_prev[k], f, from_next[k]], 0) for k, f in enumerate(fields)
+    ]
+    from_left = lax.ppermute(jnp.stack([e[:, -1:] for e in ext_y]), "col", down_cols)
+    from_right = lax.ppermute(jnp.stack([e[:, :1] for e in ext_y]), "col", up_cols)
+    return [
+        jnp.concatenate([from_left[k], e, from_right[k]], 1) for k, e in enumerate(ext_y)
+    ]
 
 
 def on_device(
@@ -211,12 +233,8 @@
     rows = lax.axis_size("row")
     col_index = lax.axis_index("col")
 
-    ext = with_halo(
-        jnp.stack(
-            [efield_x, efield_y, efield_z, hfield_x, hfield_y, hfield_z, permittivity, conductivity]
-        ),
-        (("row", 1), ("col", 2)),
-        1,
+    ext = field_halos(
+        [efield_x, efield_y, efield_z, hfield_x, hfield_y, hfield_z, permittivity, conductivity]
     )
     inside = inside_mask(count_y, count_z)
     ex_e, ey_e, ez_e = ext[0], ext[1], ext[2]
@@ -272,42 +290,52 @@
     half_ez_e = solve_local(source_z, coup_e[ys, za], 2)
     half_ez_e = jnp.where(inside[ys, za], half_ez_e, 0.0)
 
+    half_hy_e = hy_e[ys, za] + HALF_STEP * (diff_up(half_ez_e, 2) - dpz_ex)
+    half_hy_e = jnp.where(inside[ys, za], half_hy_e, 0.0)
+    dz_half_ey = half_ey_e[:, 1:] - half_ey_e[:, :-1]
+    half_hx_e = hx_e[ya, za] + HALF_STEP * (dz_half_ey[:, 0 : count_z + 1] - dpy_ez)
+    half_hx_e = jnp.where(inside[ya, za], half_hx_e, 0.0)
+
+    half_ey = half_ey_e[1 : count_y + 1, 1 : count_z + 1]
+    half_ez = half_ez_e[:, 1:]
+    dx_half_ez = diff_up(half_ez_e, 2)
+    dz_ey_own = dz_half_ey[:, 1 : count_z + 1]
+    second_z = keep * half_ez + drive * (
+        diff_down(half_hy_e[:, 1:], 2)
+        - (half_hx_e[1:, 1:] - half_hx_e[:-1, 1:])
+        - HALF_STEP * (dz_ey_own[1:] - dz_ey_own[:-1])
+    )
+
     system = RowSystem(coupling)
-    bwd_src, head_src, tail_src = system.reduce_source(source_x)
+    bwd_x, head_x, tail_x = system.reduce_source(source_x)
+    bwd_z, head_z, tail_z = system.reduce_source(second_z)
     parts = rows
     payload = jnp.stack(
         [
-            jnp.stack(system.head + [head_src]),
-            jnp.stack(system.tail + [tail_src]),
+            jnp.stack(system.head + [head_x, head_z]),
+            jnp.stack(system.tail + [tail_x, tail_z]),
         ],
         1,
     )
     payload = to_solver(payload, parts)
     received = lax.all_to_all(payload, "row", split_axis=0, concat_axis=0, tiled=True)
     width = received.shape[-1]
-    received = jnp.transpose(received, (1, 0, 2, 3)).reshape((4, parts * 2, width))
-    matrix = received[:3]
-    answer = reduced_solve(matrix, received[3], True)
+    received = jnp.transpose(received, (1, 0, 2, 3)).reshape((5, parts * 2, width))
+    answer = reduced_solve(received[:3], received[3:], True)
     back = lax.all_to_all(answer, "row", split_axis=0, concat_axis=0, tiled=True)
     bounds = from_solver(back, count_z, count_x)
-    half_ex_rows = system.expand(bwd_src, bounds[0], bounds[1])
-    half_ex_e = jnp.stack([bounds[3]] + half_ex_rows + [bounds[2]])
-
-    inside_e = inside
+    half_ex_rows = system.expand(bwd_x, bounds[0], bounds[1])
+    half_ex_e = jnp.stack([bounds[6]] + half_ex_rows + [bounds[4]])
+    next_ez_rows = system.expand(bwd_z, bounds[2], bounds[3])
+    next_ez = jnp.stack(next_ez_rows)
+    next_ez_e = jnp.stack(next_ez_rows + [bounds[5]])
+
     half_hz_e = hz_e[ya, zs] + HALF_STEP * (
         (half_ex_e[1:] - half_ex_e[:-1]) - diff_up(ey_e[ya, zs], 2)
     )
-    half_hz_e = jnp.where(inside_e[ya, zs], half_hz_e, 0.0)
-    half_hy_e = hy_e[ys, za] + HALF_STEP * (diff_up(half_ez_e, 2) - dpz_ex)
-    half_hy_e = jnp.where(inside_e[ys, za], half_hy_e, 0.0)
-    dz_half_ey = half_ey_e[:, 1:] - half_ey_e[:, :-1]
-    half_hx_e = hx_e[ya, za] + HALF_STEP * (dz_half_ey[:, 0 : count_z + 1] - dpy_ez)
-    half_hx_e = jnp.where(inside_e[ya, za], half_hx_e, 0.0)
+    half_hz_e = jnp.where(inside[ya, zs], half_hz_e, 0.0)
 
     half_ex = half_ex_e[1 : count_y + 1]
-    half_ey = half_ey_e[1 : count_y + 1, 1 : count_z + 1]
-    half_ez = half_ez_e[:, 1:]
-    dx_half_ez = diff_up(half_ez_e, 2)
     dy_half_ex = half_ex_e[2:] - half_ex_e[1:-1]
     second_x = keep * half_ex + drive * (
         (half_hz_e[1:] - half_hz_e[:-1])
@@ -319,12 +347,6 @@
         - diff_down(half_hz_e[1:], 2)
         - HALF_STEP * diff_down(dy_half_ex, 2)
     )
-    dz_ey_own = dz_half_ey[:, 1 : count_z + 1]
-    second_z = keep * half_ez + drive * (
-        diff_down(half_hy_e[:, 1:], 2)
-        - (half_hx_e[1:, 1:] - half_hx_e[:-1, 1:])
-        - HALF_STEP * (dz_ey_own[1:] - dz_ey_own[:-1])
-    )
 
     second_full = lax.all_gather(second_x, "col", axis=1, tiled=True)
     next_ex_full = solve_local(second_full, coup_full[1:], 1)
@@ -333,16 +355,6 @@
     next_ex = next_ex_e[:, :-1]
 
     next_ey = solve_local(second_y, coupling, 2)
-
-    bwd_src, head_src, tail_src = system.reduce_source(second_z)
-    payload = to_solver(jnp.stack([head_src, tail_src]), parts)
-    received = lax.all_to_all(payload, "row", split_axis=0, concat_axis=0, tiled=True)
-    answer = reduced_solve(matrix, received.reshape((parts * 2, width)), False)
-    back = lax.all_to_all(answer, "row", split_axis=0, concat_axis=0, tiled=True)
-    bounds = from_solver(back, count_z, count_x)
-    next_ez_rows = system.expand(bwd_src, bounds[0], bounds[1])
-    next_ez = jnp.stack(next_ez_rows)
-    next_ez_e = jnp.stack(next_ez_rows + [bounds[2]])
 
     next_hx = half_hx_e[1:, 1:] + HALF_STEP * (
         dz_ey_own[1:] - (next_ez_e[1:] - next_ez_e[:-1])

time: 158 us -> 130 us (0.82)
  waiting for transfers between devices: 39.1 us -> 25.2 us
  starting transfers between devices: 49.3 us -> 40.8 us
  blocking collectives: 20 us -> 16.9 us
    all_to_all x2 -> x1, waiting for transfers between devices: 18.7 us -> 11.2 us  [on_device(): lax.all_to_all(answer, 'row', split_axis=0, concat_axis=0, tiled=True)]
    all_to_all x2 -> x1, waiting for transfers between devices: 17.8 us -> 11.6 us  [on_device(): lax.all_to_all(payload, 'row', split_axis=0, concat_axis=0, tiled=True)]
    all_to_all x2 -> x1, starting transfers between devices: 26.5 us -> 21.9 us  [on_device(): lax.all_to_all(payload, 'row', split_axis=0, concat_axis=0, tiled=True)]
    all_to_all x2 -> x1, starting transfers between devices: 9.31 us -> 5.48 us  [on_device(): lax.all_to_all(answer, 'row', split_axis=0, concat_axis=0, tiled=True)]
    all_gather x1, blocking collectives: 11 us -> 7.89 us  [on_device(): second_full = lax.all_gather(second_x, 'col', axis=1, tiled=True)]
    unnamed x2 -> x13, other arithmetic: 0.79 us -> 2.82 us
    slice x80 -> x79, local copies, waits for them, and re-layouts: 4.16 us -> 3.55 us  [shifted(): lax.slice_in_dim(values, 0, length - stride, axis=line_axis)]
    unnamed x62 -> x82, local copies, waits for them, and re-layouts: 10.7 us -> 11.1 us
  transfers between devices with their start and end apart: 8 -> 6, of which waited for: 7 -> 5; matrix products, arithmetic and copies ran while one was open for 5% -> 1% of each run, Pallas kernels for 0% -> 0%
where the time goes in v1:
time: 130 us; the launch traced here: 129 us
  starting transfers between devices  40.8 us (31%)
  waiting for transfers between devices  25.2 us (19%)
  local copies, waits for them, and re-layouts  22.9 us (18%)
  other arithmetic  21 us (16%)
  blocking collectives  16.9 us (13%)
  between operations  2.64 us (2%)
    all_to_all x1, starting transfers between devices, on_device(): lax.all_to_all(payload, 'row', split_axis=0, concat_axis=0, tiled=True)  21.9 us
    all_to_all x1, waiting for transfers between devices, on_device(): lax.all_to_all(payload, 'row', split_axis=0, concat_axis=0, tiled=True)  11.6 us
    all_to_all x1, waiting for transfers between devices, on_device(): lax.all_to_all(answer, 'row', split_axis=0, concat_axis=0, tiled=True)  11.2 us
    unnamed x82, local copies, waits for them, and re-layouts  11.1 us
    all_gather x1, blocking collectives, on_device(): lax.all_gather(jnp.stack([source_y, coup_e[ya, zs]]), 'col', axis=2, tile...  9.03 us
    all_gather x1, blocking collectives, on_device(): second_full = lax.all_gather(second_x, 'col', axis=1, tiled=True)  7.89 us
    sub x30, other arithmetic, reduce_lines(): source = source - src_lo * ratio_lo - src_hi * ratio_hi  5.79 us
    ppermute x1, starting transfers between devices, field_halos(): lax.ppermute(jnp.stack([e[:, :1] for e in ext_y]), 'col', up_cols)  5.67 us
  transfers between devices with their start and end apart: 6, of which 5 were waited for; matrix products, arithmetic and copies ran while one was open for 1% of the time, Pallas kernels for 0%

profile of v1, /device:TPU:1, one launch (start us, length us, event | category | flops | bytes accessed | tf_op | source)
XLA Modules:
  0.0 129.5 jit_solution(9237288701801208480)
XLA Ops:
  0.7 0.8 constant_dynamic-update-slice_fusion.7
  1.5 0.8 copy-done.6
  2.4 0.8 copy-done.1
  3.2 0.8 copy-done.3
  4.0 1.3 collective-permute-start.1
  5.3 4.6 %collective-permute-start = (f32[8,1,8,512]{3,2,1,0:T(8,128)S(1)}, f32[8,1,8,512]{3,2,1,0:T(8,128)S(1)}, u32[]{:S(2)}, u32[]{:S(2)}) collective-permute-start(f32[8,1,8,512]{3,2,1,0:T(8,128)S(1)} %get-tuple-element.469), channel_id=1, source_target_pairs={{0,4},{4,8},{8,12},{12,16},{16,20},{20,24},{24,28},{28,32},{32,36}... | collective-permute-start | bytes 393224 | tf_op jit(solution)/shard_map/ppermute | solution.py:215
  10.8 1.0 collective-permute-done
  12.1 5.7 %collective-permute-start.3 = (f32[8,6,1,512]{3,2,1,0:T(1,128)S(1)}, f32[8,6,1,512]{3,2,1,0:T(1,128)S(1)}, u32[]{:S(2)}, u32[]{:S(2)}) collective-permute-start(f32[8,6,1,512]{3,2,1,0:T(1,128)S(1)} %get-tuple-element.340), channel_id=1, source_target_pairs={{1,0},{2,1},{3,2},{5,4},{6,5},{7,6},{9,8},{10,9},{11,10},{13,12},{... | collective-permute-start | bytes 294920 | tf_op jit(solution)/shard_map/ppermute | solution.py:221
  17.7 1.9 %collective-permute-start.2 = (f32[8,6,1,512]{3,2,1,0:T(1,128)S(1)}, f32[8,6,1,512]{3,2,1,0:T(1,128)S(1)}, u32[]{:S(2)}, u32[]{:S(2)}) collective-permute-start(f32[8,6,1,512]{3,2,1,0:T(1,128)S(1)} %get-tuple-element.341), channel_id=1, source_target_pairs={{0,1},{1,2},{2,3},{4,5},{5,6},{6,7},{8,9},{9,10},{10,11},{12,13},{... | collective-permute-start | bytes 294920 | tf_op jit(solution)/shard_map/ppermute | solution.py:220
  19.8 1.4 %collective-permute-done.3 = f32[8,6,1,512]{3,2,1,0:T(1,128)S(1)} collective-permute-done((f32[8,6,1,512]{3,2,1,0:T(1,128)S(1)}, f32[8,6,1,512]{3,2,1,0:T(1,128)S(1)}, u32[]{:S(2)}, u32[]{:S(2)}) %collective-permute-start.3) | collective-permute-done | bytes 98336 | tf_op jit(solution)/shard_map/ppermute | solution.py:221
  21.9 9.0 %all_gather.6 = f32[2,5,32,512]{3,2,1,0:T(8,128)S(1)} all-gather(f32[2,5,8,512]{3,2,1,0:T(8,128)S(1)} %pad_maximum_fusion.1), channel_id=1, replica_groups=mesh['row'=64,'col'=4] {'col'}, dimensions={2}, use_global_device_ids=true | all-gather | bytes 819200 | tf_op jit(solution)/shard_map/all_gather | solution.py:276
  44.5 1.0 reshape.257
  45.5 21.9 %all-to-all-start = ((f32[64,1,640]{2,1,0:T(1,128)}), f32[64,1,640]{2,1,0:T(1,128)S(1)}, u32[]{:S(2)}, u32[]{:S(2)}) async-start(f32[64,1,640]{2,1,0:T(1,128)} %reshape.257), calls=%async_computation | async-start | bytes 327680 | tf_op jit(solution)/shard_map/all_to_all | solution.py:321
  67.6 11.6 %all-to-all-done = f32[64,1,640]{2,1,0:T(1,128)S(1)} async-done(((f32[64,1,640]{2,1,0:T(1,128)}), f32[64,1,640]{2,1,0:T(1,128)S(1)}, u32[]{:S(2)}, u32[]{:S(2)}) %all-to-all-start) | async-done | bytes 163872 | tf_op jit(solution)/shard_map/all_to_all | solution.py:321
  79.7 1.0 reduce.28
  83.2 0.8 reshape.259
  84.1 5.5 %all-to-all-start.1 = ((f32[64,1,448]{2,1,0:T(1,128)}), f32[64,1,448]{2,1,0:T(1,128)S(1)}, u32[]{:S(2)}, u32[]{:S(2)}) async-start(f32[64,1,448]{2,1,0:T(1,128)} %reshape.259), calls=%async_computation.1 | async-start | bytes 262144 | tf_op jit(solution)/shard_map/all_to_all | solution.py:325
  89.6 11.2 %all-to-all-done.1 = f32[64,1,448]{2,1,0:T(1,128)S(1)} async-done(((f32[64,1,448]{2,1,0:T(1,128)}), f32[64,1,448]{2,1,0:T(1,128)S(1)}, u32[]{:S(2)}, u32[]{:S(2)}) %all-to-all-start.1) | async-done | bytes 114720 | tf_op jit(solution)/shard_map/all_to_all | solution.py:325
  100.8 1.0 reduce.29
  101.8 1.2 slice_reduce_fusion
  105.5 1.4 %constant_dynamic-update-slice_fusion.49 = (f32[5,8,512]{2,1,0:T(8,128)}, f32[1,8,512]{2,1,0:T(8,128)S(1)}, f32[1,8,512]{2,1,0:T(8,128)S(1)}) fusion(f32[5,8,512]{2,1,0:T(8,128)} %constant_dynamic-update-slice_fusion.50, f32[1,8,512]{2,1,0:T(8,128)S(1)} %squeeze.148, f32[1,8,512]{2,1,0:T(8,128)S(1)} %copy-done.13, f32[1,8,512]{2,1,0:T(8,128)S(1)} %get-tuple-element.91, ...), kind=kLoop, calls=%fused_computation.208 | loop fusion | flops 65536 | bytes 245760
  108.8 1.0 add_select_fusion.2
  115.6 0.7 multiply_add_fusion
  116.3 7.9 %all_gather.7 = f32[4,32,512]{2,1,0:T(8,128)S(1)} all-gather(f32[4,8,512]{2,1,0:T(8,128)S(1)} %get-tuple-element.357), channel_id=1, replica_groups=mesh['row'=64,'col'=4] {'col'}, dimensions={1}, use_global_device_ids=true | all-gather | bytes 327680 | tf_op jit(solution)/shard_map/all_gather | solution.py:351
  (380 shorter events, 32.8 us)
Async XLA Ops:
  0.6 0.8 copy-start.5
  0.6 0.9 copy-start.9
  1.5 0.8 copy-start.6
  1.5 0.8 copy-start.4
  2.3 0.8 copy-start.1
  2.4 0.8 copy-start.2
  3.2 0.8 copy-start.3
  4.0 6.8 %collective-permute-start.1 = (f32[8,1,8,512]{3,2,1,0:T(8,128)S(1)}, f32[8,1,8,512]{3,2,1,0:T(8,128)S(1)}, u32[]{:S(2)}, u32[]{:S(2)}) collective-permute-start(f32[8,1,8,512]{3,2,1,0:T(8,128)S(1)} %get-tuple-element.470), channel_id=1, source_target_pairs={{4,0},{8,4},{12,8},{16,12},{20,16},{24,20},{28,24},{32,28},{36,32}... | collective-permute-start | bytes 393224 | tf_op jit(solution)/shard_map/ppermute | solution.py:216
  5.3 6.5 %collective-permute-start = (f32[8,1,8,512]{3,2,1,0:T(8,128)S(1)}, f32[8,1,8,512]{3,2,1,0:T(8,128)S(1)}, u32[]{:S(2)}, u32[]{:S(2)}) collective-permute-start(f32[8,1,8,512]{3,2,1,0:T(8,128)S(1)} %get-tuple-element.469), channel_id=1, source_target_pairs={{0,4},{4,8},{8,12},{12,16},{16,20},{20,24},{24,28},{28,32},{32,36}... | collective-permute-start | bytes 393224 | tf_op jit(solution)/shard_map/ppermute | solution.py:215
  9.9 21.3 %copy-start.29 = (pred[32]{0:T(512)(128)(4,1)}, pred[32]{0:T(512)(128)(4,1)S(1)}, u32[]{:S(2)}) copy-start(pred[32]{0:T(512)(128)(4,1)S(1)} %get-tuple-element.497) | copy-start | bytes 100
  9.9 57.5 %copy-start.22 = (pred[32]{0:T(512)(128)(4,1)}, pred[32]{0:T(512)(128)(4,1)S(1)}, u32[]{:S(2)}) copy-start(pred[32]{0:T(512)(128)(4,1)S(1)} %get-tuple-element.498) | copy-start | bytes 100
  10.1 25.3 %copy-start.27 = (pred[512]{0:T(512)(128)(4,1)}, pred[512]{0:T(512)(128)(4,1)S(1)}, u32[]{:S(2)}) copy-start(pred[512]{0:T(512)(128)(4,1)S(1)} %get-tuple-element.499) | copy-start | bytes 1540
  10.1 25.8 %copy-start.24 = (pred[512]{0:T(512)(128)(4,1)}, pred[512]{0:T(512)(128)(4,1)S(1)}, u32[]{:S(2)}) copy-start(pred[512]{0:T(512)(128)(4,1)S(1)} %get-tuple-element.500) | copy-start | bytes 1540
  10.8 1.0 copy-start
  12.1 9.1 %collective-permute-start.3 = (f32[8,6,1,512]{3,2,1,0:T(1,128)S(1)}, f32[8,6,1,512]{3,2,1,0:T(1,128)S(1)}, u32[]{:S(2)}, u32[]{:S(2)}) collective-permute-start(f32[8,6,1,512]{3,2,1,0:T(1,128)S(1)} %get-tuple-element.340), channel_id=1, source_target_pairs={{1,0},{2,1},{3,2},{5,4},{6,5},{7,6},{9,8},{10,9},{11,10},{13,12},{... | collective-permute-start | bytes 294920 | tf_op jit(solution)/shard_map/ppermute | solution.py:221
  17.7 3.5 %collective-permute-start.2 = (f32[8,6,1,512]{3,2,1,0:T(1,128)S(1)}, f32[8,6,1,512]{3,2,1,0:T(1,128)S(1)}, u32[]{:S(2)}, u32[]{:S(2)}) collective-permute-start(f32[8,6,1,512]{3,2,1,0:T(1,128)S(1)} %get-tuple-element.341), channel_id=1, source_target_pairs={{0,1},{1,2},{2,3},{4,5},{5,6},{6,7},{8,9},{9,10},{10,11},{12,13},{... | collective-permute-start | bytes 294920 | tf_op jit(solution)/shard_map/ppermute | solution.py:220
  35.0 7.9 %copy-start.8 = (f32[4,8,512]{2,1,0:T(8,128)}, f32[4,8,512]{2,1,0:T(8,128)S(1)}, u32[]{:S(2)}) copy-start(f32[4,8,512]{2,1,0:T(8,128)S(1)} %get-tuple-element.220) | copy-start | bytes 196612
  42.5 1.1 copy-start.10
  45.5 33.6 %all-to-all-start = ((f32[64,1,640]{2,1,0:T(1,128)}), f32[64,1,640]{2,1,0:T(1,128)S(1)}, u32[]{:S(2)}, u32[]{:S(2)}) async-start(f32[64,1,640]{2,1,0:T(1,128)} %reshape.257), calls=%async_computation | async-start | bytes 327680 | tf_op jit(solution)/shard_map/all_to_all | solution.py:321
  84.1 16.7 %all-to-all-start.1 = ((f32[64,1,448]{2,1,0:T(1,128)}), f32[64,1,448]{2,1,0:T(1,128)S(1)}, u32[]{:S(2)}, u32[]{:S(2)}) async-start(f32[64,1,448]{2,1,0:T(1,128)} %reshape.259), calls=%async_computation.1 | async-start | bytes 262144 | tf_op jit(solution)/shard_map/all_to_all | solution.py:325
  103.0 0.8 copy-start.20
  103.0 2.3 %copy-start.17 = (f32[1,8,512]{2,1,0:T(8,128)S(1)}, f32[1,8,512]{2,1,0:T(8,128)}, u32[]{:S(2)}) copy-start(f32[1,8,512]{2,1,0:T(8,128)} %copy-done.16) | copy-start | bytes 49156
  103.0 2.3 %copy-start.21 = (f32[1,8,512]{2,1,0:T(8,128)S(1)}, f32[1,8,512]{2,1,0:T(8,128)}, u32[]{:S(2)}) copy-start(f32[1,8,512]{2,1,0:T(8,128)} %get-tuple-element.88) | copy-start | bytes 49156
  105.5 1.4 %copy-start.19 = (f32[1,8,512]{2,1,0:T(8,128)S(1)}, f32[1,8,512]{2,1,0:T(8,128)}, u32[]{:S(2)}) copy-start(f32[1,8,512]{2,1,0:T(8,128)} %copy-done.18) | copy-start | bytes 49156
  (13 other events, 8.4 us)

commit v2 on v1

--- a/solution.py
+++ b/solution.py
@@ -205,6 +205,61 @@
     return jnp.stack(outs, 1)
 
 
+def shift_rows(values, distance, filler):
+    rows = lax.axis_size("row")
+    step = abs(distance)
+    if distance > 0:
+        pairs = [(i, i + step) for i in range(rows - step)]
+    else:
+        pairs = [(i + step, i) for i in range(rows - step)]
+    moved = lax.ppermute(values, "row", pairs)
+    if filler is None:
+        return moved
+    row_index = lax.axis_index("row")
+    valid = (row_index - distance >= 0) & (row_index - distance < rows)
+    return jnp.where(valid, moved, filler)
+
+
+def distributed_reduce(sub, main, sup, src):
+    rows = lax.axis_size("row")
+    nrhs = src.shape[0]
+    stride = 1
+    while stride < 2 * rows:
+        if stride == 1:
+            to_next = jnp.concatenate([jnp.stack([sub[1], main[1], sup[1]]), src[:, 1]], 0)
+            to_prev = jnp.concatenate([jnp.stack([sub[0], main[0], sup[0]]), src[:, 0]], 0)
+            got_prev = shift_rows(to_next, 1, None)
+            got_next = shift_rows(to_prev, -1, None)
+            valid_prev = lax.axis_index("row") >= 1
+            valid_next = lax.axis_index("row") < rows - 1
+            sub_lo = jnp.stack([got_prev[0], sub[0]])
+            mid_lo = jnp.stack([jnp.where(valid_prev, got_prev[1], 1.0), main[0]])
+            sup_lo = jnp.stack([got_prev[2], sup[0]])
+            src_lo = jnp.stack([got_prev[3:], src[:, 0]], 1)
+            sub_hi = jnp.stack([sub[1], got_next[0]])
+            mid_hi = jnp.stack([main[1], jnp.where(valid_next, got_next[1], 1.0)])
+            sup_hi = jnp.stack([sup[1], got_next[2]])
+            src_hi = jnp.stack([src[:, 1], got_next[3:]], 1)
+        else:
+            dist = stride // 2
+            packed = jnp.concatenate([jnp.stack([sub, main, sup]), src], 0)
+            got_prev = shift_rows(packed, dist, None)
+            got_next = shift_rows(packed, -dist, None)
+            row_index = lax.axis_index("row")
+            sub_lo, sup_lo, src_lo = got_prev[0], got_prev[2], got_prev[3:]
+            mid_lo = jnp.where(row_index >= dist, got_prev[1], 1.0)
+            sub_hi, sup_hi, src_hi = got_next[0], got_next[2], got_next[3:]
+            mid_hi = jnp.where(row_index < rows - dist, got_next[1], 1.0)
+        ratio_lo = sub / mid_lo
+        ratio_hi = sup / mid_hi
+        sub = -sub_lo * ratio_lo
+        sup = -sup_hi * ratio_hi
+        main = main - sup_lo * ratio_lo - sub_hi * ratio_hi
+        src = src - src_lo * ratio_lo - src_hi * ratio_hi
+        stride = stride * 2
+    return src / main
+
+
 def field_halos(fields):
     rows = lax.axis_size("row")
     cols = lax.axis_size("col")
@@ -309,21 +364,18 @@
     system = RowSystem(coupling)
     bwd_x, head_x, tail_x = system.reduce_source(source_x)
     bwd_z, head_z, tail_z = system.reduce_source(second_z)
-    parts = rows
-    payload = jnp.stack(
-        [
-            jnp.stack(system.head + [head_x, head_z]),
-            jnp.stack(system.tail + [tail_x, tail_z]),
-        ],
-        1,
-    )
-    payload = to_solver(payload, parts)
-    received = lax.all_to_all(payload, "row", split_axis=0, concat_axis=0, tiled=True)
-    width = received.shape[-1]
-    received = jnp.transpose(received, (1, 0, 2, 3)).reshape((5, parts * 2, width))
-    answer = reduced_solve(received[:3], received[3:], True)
-    back = lax.all_to_all(answer, "row", split_axis=0, concat_axis=0, tiled=True)
-    bounds = from_solver(back, count_z, count_x)
+    solved = distributed_reduce(
+        jnp.stack([system.head[0], system.tail[0]]),
+        jnp.stack([system.head[1], system.tail[1]]),
+        jnp.stack([system.head[2], system.tail[2]]),
+        jnp.stack([jnp.stack([head_x, tail_x]), jnp.stack([head_z, tail_z])]),
+    )
+    prev_tail = shift_rows(solved[0, 1], 1, None)
+    next_heads = shift_rows(solved[:, 0], -1, None)
+    bounds = [
+        solved[0, 0], solved[0, 1], solved[1, 0], solved[1, 1],
+        next_heads[0], next_heads[1], prev_tail,
+    ]
     half_ex_rows = system.expand(bwd_x, bounds[0], bounds[1])
     half_ex_e = jnp.stack([bounds[6]] + half_ex_rows + [bounds[4]])
     next_ez_rows = system.expand(bwd_z, bounds[2], bounds[3])

time: 130 us -> 201 us (1.55)
  the two profiles are of different devices: /device:TPU:1 before, /device:TPU:95 now
where the time goes in v2:
time: 201 us; the launch traced here: 200 us
  starting transfers between devices  74.5 us (37%)
  waiting for transfers between devices  67.5 us (34%)
  blocking collectives  29.7 us (15%)
  other arithmetic  14.9 us (7%)
  local copies, waits for them, and re-layouts  10.9 us (5%)
  between operations  2.5 us (1%)
    ppermute x16, waiting for transfers between devices, shift_rows(): moved = lax.ppermute(values, 'row', pairs)  61.2 us
    ppermute x16, starting transfers between devices, shift_rows(): moved = lax.ppermute(values, 'row', pairs)  57.4 us
    all_gather x1, blocking collectives, on_device(): second_full = lax.all_gather(second_x, 'col', axis=1, tiled=True)  20.6 us
    ppermute x1, starting transfers between devices, field_halos(): lax.ppermute(jnp.stack([f[-1:] for f in fields]), 'row', down_rows)  9.15 us
    all_gather x1, blocking collectives, on_device(): lax.all_gather(jnp.stack([source_y, coup_e[ya, zs]]), 'col', axis=2, tile...  9.03 us
    sub x24, other arithmetic, reduce_lines(): source = source - src_lo * ratio_lo - src_hi * ratio_hi  5.56 us
  transfers between devices with their start and end apart: 20, of which 18 were waited for; matrix products, arithmetic and copies ran while one was open for 0% of the time, Pallas kernels for 0%

profile of v2, /device:TPU:95, one launch (start us, length us, event | category | flops | bytes accessed | tf_op | source)
XLA Modules:
  0.0 200.1 jit_solution(5800476829216050008)
XLA Ops:
  4.0 2.4 %collective-permute-start.1 = (f32[8,1,8,512]{3,2,1,0:T(8,128)S(1)}, f32[8,1,8,512]{3,2,1,0:T(8,128)S(1)}, u32[]{:S(2)}, u32[]{:S(2)}) collective-permute-start(f32[8,1,8,512]{3,2,1,0:T(8,128)S(1)} %get-tuple-element.432), channel_id=1, source_target_pairs={{4,0},{8,4},{12,8},{16,12},{20,16},{24,20},{28,24},{32,28},{36,32}... | collective-permute-start | bytes 393224 | tf_op jit(solution)/shard_map/ppermute | solution.py:271
  6.5 9.2 %collective-permute-start = (f32[8,1,8,512]{3,2,1,0:T(8,128)S(1)}, f32[8,1,8,512]{3,2,1,0:T(8,128)S(1)}, u32[]{:S(2)}, u32[]{:S(2)}) collective-permute-start(f32[8,1,8,512]{3,2,1,0:T(8,128)S(1)} %get-tuple-element.431), channel_id=1, source_target_pairs={{0,4},{4,8},{8,12},{12,16},{16,20},{20,24},{24,28},{28,32},{32,36}... | collective-permute-start | bytes 393224 | tf_op jit(solution)/shard_map/ppermute | solution.py:270
  15.9 2.1 %collective-permute-done.1 = f32[8,1,8,512]{3,2,1,0:T(8,128)S(1)} collective-permute-done((f32[8,1,8,512]{3,2,1,0:T(8,128)S(1)}, f32[8,1,8,512]{3,2,1,0:T(8,128)S(1)}, u32[]{:S(2)}, u32[]{:S(2)}) %collective-permute-start.1) | collective-permute-done | bytes 131104 | tf_op jit(solution)/shard_map/ppermute | solution.py:271
  18.0 2.7 %collective-permute-done = f32[8,1,8,512]{3,2,1,0:T(8,128)S(1)} collective-permute-done((f32[8,1,8,512]{3,2,1,0:T(8,128)S(1)}, f32[8,1,8,512]{3,2,1,0:T(8,128)S(1)}, u32[]{:S(2)}, u32[]{:S(2)}) %collective-permute-start) | collective-permute-done | bytes 131104 | tf_op jit(solution)/shard_map/ppermute | solution.py:270
  21.0 3.2 %collective-permute-start.3 = (f32[8,6,1,512]{3,2,1,0:T(1,128)S(1)}, f32[8,6,1,512]{3,2,1,0:T(1,128)S(1)}, u32[]{:S(2)}, u32[]{:S(2)}) collective-permute-start(f32[8,6,1,512]{3,2,1,0:T(1,128)S(1)} %get-tuple-element.318), channel_id=1, source_target_pairs={{1,0},{2,1},{3,2},{5,4},{6,5},{7,6},{9,8},{10,9},{11,10},{13,12},{... | collective-permute-start | bytes 294920 | tf_op jit(solution)/shard_map/ppermute | solution.py:276
  24.3 2.3 %collective-permute-start.2 = (f32[8,6,1,512]{3,2,1,0:T(1,128)S(1)}, f32[8,6,1,512]{3,2,1,0:T(1,128)S(1)}, u32[]{:S(2)}, u32[]{:S(2)}) collective-permute-start(f32[8,6,1,512]{3,2,1,0:T(1,128)S(1)} %get-tuple-element.319), channel_id=1, source_target_pairs={{0,1},{1,2},{2,3},{4,5},{5,6},{6,7},{8,9},{9,10},{10,11},{12,13},{... | collective-permute-start | bytes 294920 | tf_op jit(solution)/shard_map/ppermute | solution.py:275
  28.8 9.0 %all_gather.6 = f32[2,5,32,512]{3,2,1,0:T(8,128)S(1)} all-gather(f32[2,5,8,512]{3,2,1,0:T(8,128)S(1)} %pad_maximum_fusion), channel_id=1, replica_groups=mesh['row'=64,'col'=4] {'col'}, dimensions={2}, use_global_device_ids=true | all-gather | bytes 819200 | tf_op jit(solution)/shard_map/all_gather | solution.py:331
  48.8 10.5 %collective-permute-start.4 = (f32[5,8,512]{2,1,0:T(8,128)S(1)}, f32[5,8,512]{2,1,0:T(8,128)S(1)}, u32[]{:S(2)}, u32[]{:S(2)}) collective-permute-start(f32[5,8,512]{2,1,0:T(8,128)S(1)} %pad_maximum_fusion.16), channel_id=1, source_target_pairs={{0,4},{4,8},{8,12},{12,16},{16,20},{20,24},{24,28},{28,32},{32,36}... | collective-permute-start | bytes 245768 | tf_op jit(solution)/shard_map/ppermute | solution.py:215
  61.3 12.3 %collective-permute-done.5 = f32[5,8,512]{2,1,0:T(8,128)S(1)} collective-permute-done((f32[5,8,512]{2,1,0:T(8,128)S(1)}, f32[5,8,512]{2,1,0:T(8,128)S(1)}, u32[]{:S(2)}, u32[]{:S(2)}) %collective-permute-start.5) | collective-permute-done | bytes 81952 | tf_op jit(solution)/shard_map/ppermute | solution.py:215
  75.7 3.4 %collective-permute-start.7 = (f32[5,2,8,512]{3,2,1,0:T(8,128)S(1)}, f32[5,2,8,512]{3,2,1,0:T(8,128)S(1)}, u32[]{:S(2)}, u32[]{:S(2)}) collective-permute-start(f32[5,2,8,512]{3,2,1,0:T(8,128)S(1)} %pad_maximum_fusion.1), channel_id=1, source_target_pairs={{4,0},{8,4},{12,8},{16,12},{20,16},{24,20},{28,24},{32,28},{36,32}... | collective-permute-start | bytes 491528 | tf_op jit(solution)/shard_map/ppermute | solution.py:215
  81.0 10.3 %collective-permute-done.7 = f32[5,2,8,512]{3,2,1,0:T(8,128)S(1)} collective-permute-done((f32[5,2,8,512]{3,2,1,0:T(8,128)S(1)}, f32[5,2,8,512]{3,2,1,0:T(8,128)S(1)}, u32[]{:S(2)}, u32[]{:S(2)}) %collective-permute-start.7) | collective-permute-done | bytes 163872 | tf_op jit(solution)/shard_map/ppermute | solution.py:215
  93.3 4.9 %collective-permute-start.9 = (f32[5,2,8,512]{3,2,1,0:T(8,128)S(1)}, f32[5,2,8,512]{3,2,1,0:T(8,128)S(1)}, u32[]{:S(2)}, u32[]{:S(2)}) collective-permute-start(f32[5,2,8,512]{3,2,1,0:T(8,128)S(1)} %pad_maximum_fusion.2), channel_id=1, source_target_pairs={{8,0},{12,4},{16,8},{20,12},{24,16},{28,20},{32,24},{36,28},{40,32... | collective-permute-start | bytes 491528 | tf_op jit(solution)/shard_map/ppermute | solution.py:215
  99.6 7.2 %collective-permute-done.9 = f32[5,2,8,512]{3,2,1,0:T(8,128)S(1)} collective-permute-done((f32[5,2,8,512]{3,2,1,0:T(8,128)S(1)}, f32[5,2,8,512]{3,2,1,0:T(8,128)S(1)}, u32[]{:S(2)}, u32[]{:S(2)}) %collective-permute-start.9) | collective-permute-done | bytes 163872 | tf_op jit(solution)/shard_map/ppermute | solution.py:215
  108.8 3.4 %collective-permute-start.11 = (f32[5,2,8,512]{3,2,1,0:T(8,128)S(1)}, f32[5,2,8,512]{3,2,1,0:T(8,128)S(1)}, u32[]{:S(2)}, u32[]{:S(2)}) collective-permute-start(f32[5,2,8,512]{3,2,1,0:T(8,128)S(1)} %pad_maximum_fusion.3), channel_id=1, source_target_pairs={{16,0},{20,4},{24,8},{28,12},{32,16},{36,20},{40,24},{44,28},{48,3... | collective-permute-start | bytes 491528 | tf_op jit(solution)/shard_map/ppermute | solution.py:215
  112.9 6.3 %collective-permute-done.11 = f32[5,2,8,512]{3,2,1,0:T(8,128)S(1)} collective-permute-done((f32[5,2,8,512]{3,2,1,0:T(8,128)S(1)}, f32[5,2,8,512]{3,2,1,0:T(8,128)S(1)}, u32[]{:S(2)}, u32[]{:S(2)}) %collective-permute-start.11) | collective-permute-done | bytes 163872 | tf_op jit(solution)/shard_map/ppermute | solution.py:215
  121.5 4.9 %collective-permute-start.13 = (f32[5,2,8,512]{3,2,1,0:T(8,128)S(1)}, f32[5,2,8,512]{3,2,1,0:T(8,128)S(1)}, u32[]{:S(2)}, u32[]{:S(2)}) collective-permute-start(f32[5,2,8,512]{3,2,1,0:T(8,128)S(1)} %pad_maximum_fusion.4), channel_id=1, source_target_pairs={{32,0},{36,4},{40,8},{44,12},{48,16},{52,20},{56,24},{60,28},{64,3... | collective-permute-start | bytes 491528 | tf_op jit(solution)/shard_map/ppermute | solution.py:215
  126.8 5.3 %collective-permute-done.13 = f32[5,2,8,512]{3,2,1,0:T(8,128)S(1)} collective-permute-done((f32[5,2,8,512]{3,2,1,0:T(8,128)S(1)}, f32[5,2,8,512]{3,2,1,0:T(8,128)S(1)}, u32[]{:S(2)}, u32[]{:S(2)}) %collective-permute-start.13) | collective-permute-done | bytes 163872 | tf_op jit(solution)/shard_map/ppermute | solution.py:215
  134.2 4.3 %collective-permute-start.15 = (f32[5,2,8,512]{3,2,1,0:T(8,128)S(1)}, f32[5,2,8,512]{3,2,1,0:T(8,128)S(1)}, u32[]{:S(2)}, u32[]{:S(2)}) collective-permute-start(f32[5,2,8,512]{3,2,1,0:T(8,128)S(1)} %pad_maximum_fusion.5), channel_id=1, source_target_pairs={{64,0},{68,4},{72,8},{76,12},{80,16},{84,20},{88,24},{92,28},{96,3... | collective-permute-start | bytes 491528 | tf_op jit(solution)/shard_map/ppermute | solution.py:215
  139.5 2.9 %collective-permute-done.15 = f32[5,2,8,512]{3,2,1,0:T(8,128)S(1)} collective-permute-done((f32[5,2,8,512]{3,2,1,0:T(8,128)S(1)}, f32[5,2,8,512]{3,2,1,0:T(8,128)S(1)}, u32[]{:S(2)}, u32[]{:S(2)}) %collective-permute-start.15) | collective-permute-done | bytes 163872 | tf_op jit(solution)/shard_map/ppermute | solution.py:215
  143.8 7.9 %collective-permute-start.16 = (f32[5,2,8,512]{3,2,1,0:T(8,128)S(1)}, f32[5,2,8,512]{3,2,1,0:T(8,128)S(1)}, u32[]{:S(2)}, u32[]{:S(2)}) collective-permute-start(f32[5,2,8,512]{3,2,1,0:T(8,128)S(1)} %pad_maximum_fusion.6), channel_id=1, source_target_pairs={{0,128},{4,132},{8,136},{12,140},{16,144},{20,148},{24,152},{28,15... | collective-permute-start | bytes 491528 | tf_op jit(solution)/shard_map/ppermute | solution.py:215
  151.8 2.5 %collective-permute-done.17 = f32[5,2,8,512]{3,2,1,0:T(8,128)S(1)} collective-permute-done((f32[5,2,8,512]{3,2,1,0:T(8,128)S(1)}, f32[5,2,8,512]{3,2,1,0:T(8,128)S(1)}, u32[]{:S(2)}, u32[]{:S(2)}) %collective-permute-start.17) | collective-permute-done | bytes 163872 | tf_op jit(solution)/shard_map/ppermute | solution.py:215
  157.9 3.4 %collective-permute-start.18 = (f32[2,8,512]{2,1,0:T(8,128)S(1)}, f32[2,8,512]{2,1,0:T(8,128)S(1)}, u32[]{:S(2)}, u32[]{:S(2)}) collective-permute-start(f32[2,8,512]{2,1,0:T(8,128)S(1)} %slice_bitcast_fusion.2), channel_id=1, source_target_pairs={{4,0},{8,4},{12,8},{16,12},{20,16},{24,20},{28,24},{32,28},{36,32}... | collective-permute-start | bytes 98312 | tf_op jit(solution)/shard_map/ppermute | solution.py:215
  161.4 7.5 %collective-permute-done.18 = f32[2,8,512]{2,1,0:T(8,128)S(1)} collective-permute-done((f32[2,8,512]{2,1,0:T(8,128)S(1)}, f32[2,8,512]{2,1,0:T(8,128)S(1)}, u32[]{:S(2)}, u32[]{:S(2)}) %collective-permute-start.18) | collective-permute-done | bytes 32800 | tf_op jit(solution)/shard_map/ppermute | solution.py:215
  174.9 20.6 %all_gather.7 = f32[4,32,512]{2,1,0:T(8,128)S(1)} all-gather(f32[4,8,512]{2,1,0:T(8,128)S(1)} %get-tuple-element.335), channel_id=1, replica_groups=mesh['row'=64,'col'=4] {'col'}, dimensions={1}, use_global_device_ids=true | all-gather | bytes 327680 | tf_op jit(solution)/shard_map/all_gather | solution.py:403
  (319 shorter events, 49.4 us)
Async XLA Ops:
  0.6 0.9 copy-start.8
  1.5 0.8 copy-start.6
  1.5 0.8 copy-start.4
  4.0 14.0 %collective-permute-start.1 = (f32[8,1,8,512]{3,2,1,0:T(8,128)S(1)}, f32[8,1,8,512]{3,2,1,0:T(8,128)S(1)}, u32[]{:S(2)}, u32[]{:S(2)}) collective-permute-start(f32[8,1,8,512]{3,2,1,0:T(8,128)S(1)} %get-tuple-element.432), channel_id=1, source_target_pairs={{4,0},{8,4},{12,8},{16,12},{20,16},{24,20},{28,24},{32,28},{36,32}... | collective-permute-start | bytes 393224 | tf_op jit(solution)/shard_map/ppermute | solution.py:271
  6.5 14.3 %collective-permute-start = (f32[8,1,8,512]{3,2,1,0:T(8,128)S(1)}, f32[8,1,8,512]{3,2,1,0:T(8,128)S(1)}, u32[]{:S(2)}, u32[]{:S(2)}) collective-permute-start(f32[8,1,8,512]{3,2,1,0:T(8,128)S(1)} %get-tuple-element.431), channel_id=1, source_target_pairs={{0,4},{4,8},{8,12},{12,16},{16,20},{20,24},{24,28},{28,32},{32,36}... | collective-permute-start | bytes 393224 | tf_op jit(solution)/shard_map/ppermute | solution.py:270
  18.0 2.7 %copy-start = (f32[4,8,512]{2,1,0:T(8,128)S(1)}, f32[4,8,512]{2,1,0:T(8,128)}, u32[]{:S(2)}) copy-start(f32[4,8,512]{2,1,0:T(8,128)} %param.8) | copy-start | bytes 196612
  21.0 5.9 %collective-permute-start.3 = (f32[8,6,1,512]{3,2,1,0:T(1,128)S(1)}, f32[8,6,1,512]{3,2,1,0:T(1,128)S(1)}, u32[]{:S(2)}, u32[]{:S(2)}) collective-permute-start(f32[8,6,1,512]{3,2,1,0:T(1,128)S(1)} %get-tuple-element.318), channel_id=1, source_target_pairs={{1,0},{2,1},{3,2},{5,4},{6,5},{7,6},{9,8},{10,9},{11,10},{13,12},{... | collective-permute-start | bytes 294920 | tf_op jit(solution)/shard_map/ppermute | solution.py:276
  24.3 4.0 %collective-permute-start.2 = (f32[8,6,1,512]{3,2,1,0:T(1,128)S(1)}, f32[8,6,1,512]{3,2,1,0:T(1,128)S(1)}, u32[]{:S(2)}, u32[]{:S(2)}) collective-permute-start(f32[8,6,1,512]{3,2,1,0:T(1,128)S(1)} %get-tuple-element.319), channel_id=1, source_target_pairs={{0,1},{1,2},{2,3},{4,5},{5,6},{6,7},{8,9},{9,10},{10,11},{12,13},{... | collective-permute-start | bytes 294920 | tf_op jit(solution)/shard_map/ppermute | solution.py:275
  48.8 12.5 %collective-permute-start.4 = (f32[5,8,512]{2,1,0:T(8,128)S(1)}, f32[5,8,512]{2,1,0:T(8,128)S(1)}, u32[]{:S(2)}, u32[]{:S(2)}) collective-permute-start(f32[5,8,512]{2,1,0:T(8,128)S(1)} %pad_maximum_fusion.16), channel_id=1, source_target_pairs={{0,4},{4,8},{8,12},{12,16},{16,20},{20,24},{24,28},{28,32},{32,36}... | collective-permute-start | bytes 245768 | tf_op jit(solution)/shard_map/ppermute | solution.py:215
  59.3 14.3 %collective-permute-start.5 = (f32[5,8,512]{2,1,0:T(8,128)S(1)}, f32[5,8,512]{2,1,0:T(8,128)S(1)}, u32[]{:S(2)}, u32[]{:S(2)}) collective-permute-start(f32[5,8,512]{2,1,0:T(8,128)S(1)} %pad_maximum_fusion.17), channel_id=1, source_target_pairs={{4,0},{8,4},{12,8},{16,12},{20,16},{24,20},{28,24},{32,28},{36,32}... | collective-permute-start | bytes 245768 | tf_op jit(solution)/shard_map/ppermute | solution.py:215
  73.8 7.2 %collective-permute-start.6 = (f32[5,2,8,512]{3,2,1,0:T(8,128)S(1)}, f32[5,2,8,512]{3,2,1,0:T(8,128)S(1)}, u32[]{:S(2)}, u32[]{:S(2)}) collective-permute-start(f32[5,2,8,512]{3,2,1,0:T(8,128)S(1)} %pad_maximum_fusion.1), channel_id=1, source_target_pairs={{0,4},{4,8},{8,12},{12,16},{16,20},{20,24},{24,28},{28,32},{32,36}... | collective-permute-start | bytes 491528 | tf_op jit(solution)/shard_map/ppermute | solution.py:215
  75.7 15.6 %collective-permute-start.7 = (f32[5,2,8,512]{3,2,1,0:T(8,128)S(1)}, f32[5,2,8,512]{3,2,1,0:T(8,128)S(1)}, u32[]{:S(2)}, u32[]{:S(2)}) collective-permute-start(f32[5,2,8,512]{3,2,1,0:T(8,128)S(1)} %pad_maximum_fusion.1), channel_id=1, source_target_pairs={{4,0},{8,4},{12,8},{16,12},{20,16},{24,20},{28,24},{32,28},{36,32}... | collective-permute-start | bytes 491528 | tf_op jit(solution)/shard_map/ppermute | solution.py:215
  91.4 8.2 %collective-permute-start.8 = (f32[5,2,8,512]{3,2,1,0:T(8,128)S(1)}, f32[5,2,8,512]{3,2,1,0:T(8,128)S(1)}, u32[]{:S(2)}, u32[]{:S(2)}) collective-permute-start(f32[5,2,8,512]{3,2,1,0:T(8,128)S(1)} %pad_maximum_fusion.2), channel_id=1, source_target_pairs={{0,8},{4,12},{8,16},{12,20},{16,24},{20,28},{24,32},{28,36},{32,40... | collective-permute-start | bytes 491528 | tf_op jit(solution)/shard_map/ppermute | solution.py:215
  93.3 13.4 %collective-permute-start.9 = (f32[5,2,8,512]{3,2,1,0:T(8,128)S(1)}, f32[5,2,8,512]{3,2,1,0:T(8,128)S(1)}, u32[]{:S(2)}, u32[]{:S(2)}) collective-permute-start(f32[5,2,8,512]{3,2,1,0:T(8,128)S(1)} %pad_maximum_fusion.2), channel_id=1, source_target_pairs={{8,0},{12,4},{16,8},{20,12},{24,16},{28,20},{32,24},{36,28},{40,32... | collective-permute-start | bytes 491528 | tf_op jit(solution)/shard_map/ppermute | solution.py:215
  106.8 6.1 %collective-permute-start.10 = (f32[5,2,8,512]{3,2,1,0:T(8,128)S(1)}, f32[5,2,8,512]{3,2,1,0:T(8,128)S(1)}, u32[]{:S(2)}, u32[]{:S(2)}) collective-permute-start(f32[5,2,8,512]{3,2,1,0:T(8,128)S(1)} %pad_maximum_fusion.3), channel_id=1, source_target_pairs={{0,16},{4,20},{8,24},{12,28},{16,32},{20,36},{24,40},{28,44},{32,4... | collective-permute-start | bytes 491528 | tf_op jit(solution)/shard_map/ppermute | solution.py:215
  108.8 10.3 %collective-permute-start.11 = (f32[5,2,8,512]{3,2,1,0:T(8,128)S(1)}, f32[5,2,8,512]{3,2,1,0:T(8,128)S(1)}, u32[]{:S(2)}, u32[]{:S(2)}) collective-permute-start(f32[5,2,8,512]{3,2,1,0:T(8,128)S(1)} %pad_maximum_fusion.3), channel_id=1, source_target_pairs={{16,0},{20,4},{24,8},{28,12},{32,16},{36,20},{40,24},{44,28},{48,3... | collective-permute-start | bytes 491528 | tf_op jit(solution)/shard_map/ppermute | solution.py:215
  119.3 7.6 %collective-permute-start.12 = (f32[5,2,8,512]{3,2,1,0:T(8,128)S(1)}, f32[5,2,8,512]{3,2,1,0:T(8,128)S(1)}, u32[]{:S(2)}, u32[]{:S(2)}) collective-permute-start(f32[5,2,8,512]{3,2,1,0:T(8,128)S(1)} %pad_maximum_fusion.4), channel_id=1, source_target_pairs={{0,32},{4,36},{8,40},{12,44},{16,48},{20,52},{24,56},{28,60},{32,6... | collective-permute-start | bytes 491528 | tf_op jit(solution)/shard_map/ppermute | solution.py:215
  121.5 10.7 %collective-permute-start.13 = (f32[5,2,8,512]{3,2,1,0:T(8,128)S(1)}, f32[5,2,8,512]{3,2,1,0:T(8,128)S(1)}, u32[]{:S(2)}, u32[]{:S(2)}) collective-permute-start(f32[5,2,8,512]{3,2,1,0:T(8,128)S(1)} %pad_maximum_fusion.4), channel_id=1, source_target_pairs={{32,0},{36,4},{40,8},{44,12},{48,16},{52,20},{56,24},{60,28},{64,3... | collective-permute-start | bytes 491528 | tf_op jit(solution)/shard_map/ppermute | solution.py:215
  132.2 7.3 %collective-permute-start.14 = (f32[5,2,8,512]{3,2,1,0:T(8,128)S(1)}, f32[5,2,8,512]{3,2,1,0:T(8,128)S(1)}, u32[]{:S(2)}, u32[]{:S(2)}) collective-permute-start(f32[5,2,8,512]{3,2,1,0:T(8,128)S(1)} %pad_maximum_fusion.5), channel_id=1, source_target_pairs={{0,64},{4,68},{8,72},{12,76},{16,80},{20,84},{24,88},{28,92},{32,9... | collective-permute-start | bytes 491528 | tf_op jit(solution)/shard_map/ppermute | solution.py:215
  134.2 8.2 %collective-permute-start.15 = (f32[5,2,8,512]{3,2,1,0:T(8,128)S(1)}, f32[5,2,8,512]{3,2,1,0:T(8,128)S(1)}, u32[]{:S(2)}, u32[]{:S(2)}) collective-permute-start(f32[5,2,8,512]{3,2,1,0:T(8,128)S(1)} %pad_maximum_fusion.5), channel_id=1, source_target_pairs={{64,0},{68,4},{72,8},{76,12},{80,16},{84,20},{88,24},{92,28},{96,3... | collective-permute-start | bytes 491528 | tf_op jit(solution)/shard_map/ppermute | solution.py:215
  142.5 11.8 %collective-permute-start.17 = (f32[5,2,8,512]{3,2,1,0:T(8,128)S(1)}, f32[5,2,8,512]{3,2,1,0:T(8,128)S(1)}, u32[]{:S(2)}, u32[]{:S(2)}) collective-permute-start(f32[5,2,8,512]{3,2,1,0:T(8,128)S(1)} %pad_maximum_fusion.6), channel_id=1, source_target_pairs={{128,0},{132,4},{136,8},{140,12},{144,16},{148,20},{152,24},{156,2... | collective-permute-start | bytes 491528 | tf_op jit(solution)/shard_map/ppermute | solution.py:215
  143.8 12.1 %collective-permute-start.16 = (f32[5,2,8,512]{3,2,1,0:T(8,128)S(1)}, f32[5,2,8,512]{3,2,1,0:T(8,128)S(1)}, u32[]{:S(2)}, u32[]{:S(2)}) collective-permute-start(f32[5,2,8,512]{3,2,1,0:T(8,128)S(1)} %pad_maximum_fusion.6), channel_id=1, source_target_pairs={{0,128},{4,132},{8,136},{12,140},{16,144},{20,148},{24,152},{28,15... | collective-permute-start | bytes 491528 | tf_op jit(solution)/shard_map/ppermute | solution.py:215
  155.9 5.3 %collective-permute-start.19 = (f32[8,512]{1,0:T(8,128)S(1)}, f32[8,512]{1,0:T(8,128)S(1)}, u32[]{:S(2)}, u32[]{:S(2)}) collective-permute-start(f32[8,512]{1,0:T(8,128)S(1)} %get-tuple-element.345), channel_id=1, source_target_pairs={{0,4},{4,8},{8,12},{12,16},{16,20},{20,24},{24,28},{28,32},{32,36}... | collective-permute-start | bytes 49160 | tf_op jit(solution)/shard_map/ppermute | solution.py:215
  157.9 11.0 %collective-permute-start.18 = (f32[2,8,512]{2,1,0:T(8,128)S(1)}, f32[2,8,512]{2,1,0:T(8,128)S(1)}, u32[]{:S(2)}, u32[]{:S(2)}) collective-permute-start(f32[2,8,512]{2,1,0:T(8,128)S(1)} %slice_bitcast_fusion.2), channel_id=1, source_target_pairs={{4,0},{8,4},{12,8},{16,12},{20,16},{24,20},{28,24},{32,28},{36,32}... | collective-permute-start | bytes 98312 | tf_op jit(solution)/shard_map/ppermute | solution.py:215
  (5 other events, 4.0 us)

commit v3 on v1

--- a/solution.py
+++ b/solution.py
@@ -205,6 +205,22 @@
     return jnp.stack(outs, 1)
 
 
+def gather_cols(block, axis):
+    cols = lax.axis_size("col")
+    col_index = lax.axis_index("col")
+    got = [block]
+    for shift in range(1, cols):
+        got.append(lax.ppermute(block, "col", [(i, (i + shift) % cols) for i in range(cols)]))
+    pieces = []
+    for place in range(cols):
+        shift_needed = (col_index - place) % cols
+        piece = got[0]
+        for shift in range(1, cols):
+            piece = jnp.where(shift_needed == shift, got[shift], piece)
+        pieces.append(piece)
+    return jnp.concatenate(pieces, axis)
+
+
 def field_halos(fields):
     rows = lax.axis_size("row")
     cols = lax.axis_size("col")
@@ -273,9 +289,7 @@
         - HALF_STEP * diff_down(dpz_ex, 2)
     )
 
-    gathered = lax.all_gather(
-        jnp.stack([source_y, coup_e[ya, zs]]), "col", axis=2, tiled=True
-    )
+    gathered = gather_cols(jnp.stack([source_y, coup_e[ya, zs]]), 2)
     coup_full = gathered[1]
     half_ey_full = solve_local(gathered[0], coup_full, 1)
     pos_y = (
@@ -348,7 +362,7 @@
         - HALF_STEP * diff_down(dy_half_ex, 2)
     )
 
-    second_full = lax.all_gather(second_x, "col", axis=1, tiled=True)
+    second_full = gather_cols(second_x, 1)
     next_ex_full = solve_local(second_full, coup_full[1:], 1)
     padded = jnp.pad(next_ex_full, ((0, 0), (0, 1), (0, 0)))
     next_ex_e = lax.dynamic_slice_in_dim(padded, col_index * count_z, count_z + 1, axis=1)

time: 130 us -> 124 us (0.954)
  blocking collectives: 16.9 us -> 0 us
  starting transfers between devices: 40.8 us -> 46.8 us
  local copies, waits for them, and re-layouts: 22.9 us -> 26.7 us
    all_gather x2 -> x0, blocking collectives: 16.9 us -> none  [the longest x1 9.03 us: on_device(): lax.all_gather(jnp.stack([source_y, coup_e[ya, zs]]), 'col', axis=2, tile...]
    ppermute x0 -> x6, starting transfers between devices: none -> 8.28 us  [gather_cols(): lax.ppermute(block, 'col', [(i, (i + shift) % cols) for i in range(cols)])]
    unnamed x82 -> x104, local copies, waits for them, and re-layouts: 11.1 us -> 15.1 us
  transfers between devices with their start and end apart: 6 -> 12, of which waited for: 5 -> 4; matrix products, arithmetic and copies ran while one was open for 1% -> 9% of each run, Pallas kernels for 0% -> 0%
where the time goes in v3:
time: 124 us; the launch traced here: 123 us
  starting transfers between devices  46.8 us (38%)
  local copies, waits for them, and re-layouts  26.7 us (22%)
  waiting for transfers between devices  24.6 us (20%)
  other arithmetic  21.7 us (18%)
  between operations  2.79 us (2%)
    all_to_all x1, starting transfers between devices, on_device(): lax.all_to_all(payload, 'row', split_axis=0, concat_axis=0, tiled=True)  21.1 us
    unnamed x104, local copies, waits for them, and re-layouts  15.1 us
    all_to_all x1, waiting for transfers between devices, on_device(): lax.all_to_all(answer, 'row', split_axis=0, concat_axis=0, tiled=True)  11.7 us
    all_to_all x1, waiting for transfers between devices, on_device(): lax.all_to_all(payload, 'row', split_axis=0, concat_axis=0, tiled=True)  11.4 us
    ppermute x6, starting transfers between devices, gather_cols(): lax.ppermute(block, 'col', [(i, (i + shift) % cols) for i in range(cols)])  8.28 us
    sub x30, other arithmetic, reduce_lines(): source = source - src_lo * ratio_lo - src_hi * ratio_hi  5.78 us
    ppermute x1, starting transfers between devices, field_halos(): lax.ppermute(jnp.stack([e[:, :1] for e in ext_y]), 'col', up_cols)  5.09 us
    all_to_all x1, starting transfers between devices, on_device(): lax.all_to_all(answer, 'row', split_axis=0, concat_axis=0, tiled=True)  4.61 us
  transfers between devices with their start and end apart: 12, of which 4 were waited for; matrix products, arithmetic and copies ran while one was open for 9% of the time, Pallas kernels for 0%

profile of v3, /device:TPU:1, one launch (start us, length us, event | category | flops | bytes accessed | tf_op | source)
XLA Modules:
  0.0 122.6 jit_solution(11933700103541443675)
XLA Ops:
  0.7 0.8 constant_dynamic-update-slice_fusion.7
  1.5 0.8 copy-done.6
  2.4 0.8 copy-done.1
  3.2 0.8 copy-done.3
  4.0 1.3 %collective-permute-start.1 = (f32[8,1,8,512]{3,2,1,0:T(8,128)S(1)}, f32[8,1,8,512]{3,2,1,0:T(8,128)S(1)}, u32[]{:S(2)}, u32[]{:S(2)}) collective-permute-start(f32[8,1,8,512]{3,2,1,0:T(8,128)S(1)} %get-tuple-element.477), channel_id=1, source_target_pairs={{4,0},{8,4},{12,8},{16,12},{20,16},{24,20},{28,24},{32,28},{36,32}... | collective-permute-start | bytes 393224 | tf_op jit(solution)/shard_map/ppermute | solution.py:232
  5.3 4.6 %collective-permute-start = (f32[8,1,8,512]{3,2,1,0:T(8,128)S(1)}, f32[8,1,8,512]{3,2,1,0:T(8,128)S(1)}, u32[]{:S(2)}, u32[]{:S(2)}) collective-permute-start(f32[8,1,8,512]{3,2,1,0:T(8,128)S(1)} %get-tuple-element.476), channel_id=1, source_target_pairs={{0,4},{4,8},{8,12},{12,16},{16,20},{20,24},{24,28},{28,32},{32,36}... | collective-permute-start | bytes 393224 | tf_op jit(solution)/shard_map/ppermute | solution.py:231
  12.5 0.8 copy-done
  13.5 5.1 %collective-permute-start.3 = (f32[8,6,1,512]{3,2,1,0:T(1,128)S(1)}, f32[8,6,1,512]{3,2,1,0:T(1,128)S(1)}, u32[]{:S(2)}, u32[]{:S(2)}) collective-permute-start(f32[8,6,1,512]{3,2,1,0:T(1,128)S(1)} %get-tuple-element.347), channel_id=1, source_target_pairs={{1,0},{2,1},{3,2},{5,4},{6,5},{7,6},{9,8},{10,9},{11,10},{13,12},{... | collective-permute-start | bytes 294920 | tf_op jit(solution)/shard_map/ppermute | solution.py:237
  18.6 1.9 %collective-permute-start.2 = (f32[8,6,1,512]{3,2,1,0:T(1,128)S(1)}, f32[8,6,1,512]{3,2,1,0:T(1,128)S(1)}, u32[]{:S(2)}, u32[]{:S(2)}) collective-permute-start(f32[8,6,1,512]{3,2,1,0:T(1,128)S(1)} %get-tuple-element.348), channel_id=1, source_target_pairs={{0,1},{1,2},{2,3},{4,5},{5,6},{6,7},{8,9},{9,10},{10,11},{12,13},{... | collective-permute-start | bytes 294920 | tf_op jit(solution)/shard_map/ppermute | solution.py:236
  21.2 1.0 collective-permute-done.2
  22.8 2.5 %collective-permute-start.5 = (f32[2,5,8,512]{3,2,1,0:T(8,128)S(1)}, f32[2,5,8,512]{3,2,1,0:T(8,128)S(1)}, u32[]{:S(2)}, u32[]{:S(2)}) collective-permute-start(f32[2,5,8,512]{3,2,1,0:T(8,128)S(1)} %pad_maximum_fusion.3), channel_id=1, source_target_pairs={{0,2},{1,3},{2,0},{3,1},{4,6},{5,7},{6,4},{7,5},{8,10},{9,11},{10,... | collective-permute-start | bytes 491528 | tf_op jit(solution)/shard_map/ppermute | solution.py:213
  42.6 1.0 reshape.257
  43.6 21.1 %all-to-all-start = ((f32[64,1,640]{2,1,0:T(1,128)}), f32[64,1,640]{2,1,0:T(1,128)S(1)}, u32[]{:S(2)}, u32[]{:S(2)}) async-start(f32[64,1,640]{2,1,0:T(1,128)} %reshape.257), calls=%async_computation | async-start | bytes 327680 | tf_op jit(solution)/shard_map/all_to_all | solution.py:335
  65.4 11.4 %all-to-all-done = f32[64,1,640]{2,1,0:T(1,128)S(1)} async-done(((f32[64,1,640]{2,1,0:T(1,128)}), f32[64,1,640]{2,1,0:T(1,128)S(1)}, u32[]{:S(2)}, u32[]{:S(2)}) %all-to-all-start) | async-done | bytes 163872 | tf_op jit(solution)/shard_map/all_to_all | solution.py:335
  77.3 1.0 reduce.28
  80.9 0.8 reshape.259
  81.7 4.6 %all-to-all-start.1 = ((f32[64,1,448]{2,1,0:T(1,128)}), f32[64,1,448]{2,1,0:T(1,128)S(1)}, u32[]{:S(2)}, u32[]{:S(2)}) async-start(f32[64,1,448]{2,1,0:T(1,128)} %reshape.259), calls=%async_computation.1 | async-start | bytes 262144 | tf_op jit(solution)/shard_map/all_to_all | solution.py:339
  86.4 11.7 %all-to-all-done.1 = f32[64,1,448]{2,1,0:T(1,128)S(1)} async-done(((f32[64,1,448]{2,1,0:T(1,128)}), f32[64,1,448]{2,1,0:T(1,128)S(1)}, u32[]{:S(2)}, u32[]{:S(2)}) %all-to-all-start.1) | async-done | bytes 114720 | tf_op jit(solution)/shard_map/all_to_all | solution.py:339
  98.0 1.0 reduce.29
  99.1 1.1 slice_reduce_fusion
  101.4 1.4 %constant_dynamic-update-slice_fusion.49 = (f32[5,8,512]{2,1,0:T(8,128)S(1)}, f32[1,8,512]{2,1,0:T(8,128)S(1)}, f32[1,8,512]{2,1,0:T(8,128)}) fusion(f32[5,8,512]{2,1,0:T(8,128)S(1)} %constant_dynamic-update-slice_fusion.50, f32[1,8,512]{2,1,0:T(8,128)S(1)} %squeeze.148, f32[1,8,512]{2,1,0:T(8,128)S(1)} %copy-done.14, ...), kind=kLoop, calls=%fused_computation.214 | loop fusion | flops 65536 | bytes 245760
  110.1 3.8 %collective-permute-start.7 = (f32[4,8,512]{2,1,0:T(8,128)S(1)}, f32[4,8,512]{2,1,0:T(8,128)S(1)}, u32[]{:S(2)}, u32[]{:S(2)}) collective-permute-start(f32[4,8,512]{2,1,0:T(8,128)S(1)} %get-tuple-element.364), channel_id=1, source_target_pairs={{0,3},{1,0},{2,1},{3,2},{4,7},{5,4},{6,5},{7,6},{8,11},{9,8},{10,9... | collective-permute-start | bytes 196616 | tf_op jit(solution)/shard_map/ppermute | solution.py:213
  113.9 1.6 %collective-permute-start.9 = (f32[4,8,512]{2,1,0:T(8,128)S(1)}, f32[4,8,512]{2,1,0:T(8,128)S(1)}, u32[]{:S(2)}, u32[]{:S(2)}) collective-permute-start(f32[4,8,512]{2,1,0:T(8,128)S(1)} %get-tuple-element.364), channel_id=1, source_target_pairs={{0,1},{1,2},{2,3},{3,0},{4,5},{5,6},{6,7},{7,4},{8,9},{9,10},{10,1... | collective-permute-start | bytes 196616 | tf_op jit(solution)/shard_map/ppermute | solution.py:213
  116.3 1.6 %fusion.47 = (f32[4,8,512]{2,1,0:T(8,128)}, f32[4,8,512]{2,1,0:T(8,128)}) fusion(f32[1,8,512]{2,1,0:T(8,128)S(1)} %slice.1811, f32[1,8,512]{2,1,0:T(8,128)S(1)} %copy-done.20, f32[1,8,512]{2,1,0:T(8,128)S(1)} %get-tuple-element.492, f32[1,8,512]{2,1,0:T(8,128)S(1)} %copy-done.29, f32[5,9,512]{2,1,0:T(8,128)} %copy-done.7, ...), kind=kLoop, calls=%fused_computation.276 | loop fusion | flops 163840 | bytes 344064 | tf_op jit(solution)/shard_map/add | solution.py:373
  (417 shorter events, 37.5 us)
Async XLA Ops:
  0.6 0.9 copy-start.10
  4.0 8.4 %collective-permute-start.1 = (f32[8,1,8,512]{3,2,1,0:T(8,128)S(1)}, f32[8,1,8,512]{3,2,1,0:T(8,128)S(1)}, u32[]{:S(2)}, u32[]{:S(2)}) collective-permute-start(f32[8,1,8,512]{3,2,1,0:T(8,128)S(1)} %get-tuple-element.477), channel_id=1, source_target_pairs={{4,0},{8,4},{12,8},{16,12},{20,16},{24,20},{28,24},{32,28},{36,32}... | collective-permute-start | bytes 393224 | tf_op jit(solution)/shard_map/ppermute | solution.py:232
  5.3 7.1 %collective-permute-start = (f32[8,1,8,512]{3,2,1,0:T(8,128)S(1)}, f32[8,1,8,512]{3,2,1,0:T(8,128)S(1)}, u32[]{:S(2)}, u32[]{:S(2)}) collective-permute-start(f32[8,1,8,512]{3,2,1,0:T(8,128)S(1)} %get-tuple-element.476), channel_id=1, source_target_pairs={{0,4},{4,8},{8,12},{12,16},{16,20},{20,24},{24,28},{28,32},{32,36}... | collective-permute-start | bytes 393224 | tf_op jit(solution)/shard_map/ppermute | solution.py:231
  10.7 15.5 %copy-start.37 = (pred[512]{0:T(512)(128)(4,1)}, pred[512]{0:T(512)(128)(4,1)S(1)}, u32[]{:S(2)}) copy-start(pred[512]{0:T(512)(128)(4,1)S(1)} %get-tuple-element.506) | copy-start | bytes 1540
  10.7 16.0 %copy-start.33 = (pred[512]{0:T(512)(128)(4,1)}, pred[512]{0:T(512)(128)(4,1)S(1)}, u32[]{:S(2)}) copy-start(pred[512]{0:T(512)(128)(4,1)S(1)} %get-tuple-element.507) | copy-start | bytes 1540
  13.5 7.6 %collective-permute-start.3 = (f32[8,6,1,512]{3,2,1,0:T(1,128)S(1)}, f32[8,6,1,512]{3,2,1,0:T(1,128)S(1)}, u32[]{:S(2)}, u32[]{:S(2)}) collective-permute-start(f32[8,6,1,512]{3,2,1,0:T(1,128)S(1)} %get-tuple-element.347), channel_id=1, source_target_pairs={{1,0},{2,1},{3,2},{5,4},{6,5},{7,6},{9,8},{10,9},{11,10},{13,12},{... | collective-permute-start | bytes 294920 | tf_op jit(solution)/shard_map/ppermute | solution.py:237
  18.6 3.5 %collective-permute-start.2 = (f32[8,6,1,512]{3,2,1,0:T(1,128)S(1)}, f32[8,6,1,512]{3,2,1,0:T(1,128)S(1)}, u32[]{:S(2)}, u32[]{:S(2)}) collective-permute-start(f32[8,6,1,512]{3,2,1,0:T(1,128)S(1)} %get-tuple-element.348), channel_id=1, source_target_pairs={{0,1},{1,2},{2,3},{4,5},{5,6},{6,7},{8,9},{9,10},{10,11},{12,13},{... | collective-permute-start | bytes 294920 | tf_op jit(solution)/shard_map/ppermute | solution.py:236
  22.8 9.9 %collective-permute-start.4 = (f32[2,5,8,512]{3,2,1,0:T(8,128)S(1)}, f32[2,5,8,512]{3,2,1,0:T(8,128)S(1)}, u32[]{:S(2)}, u32[]{:S(2)}) collective-permute-start(f32[2,5,8,512]{3,2,1,0:T(8,128)S(1)} %pad_maximum_fusion.3), channel_id=1, source_target_pairs={{0,3},{1,0},{2,1},{3,2},{4,7},{5,4},{6,5},{7,6},{8,11},{9,8},{10,9... | collective-permute-start | bytes 491528 | tf_op jit(solution)/shard_map/ppermute | solution.py:213
  22.8 9.8 %collective-permute-start.5 = (f32[2,5,8,512]{3,2,1,0:T(8,128)S(1)}, f32[2,5,8,512]{3,2,1,0:T(8,128)S(1)}, u32[]{:S(2)}, u32[]{:S(2)}) collective-permute-start(f32[2,5,8,512]{3,2,1,0:T(8,128)S(1)} %pad_maximum_fusion.3), channel_id=1, source_target_pairs={{0,2},{1,3},{2,0},{3,1},{4,6},{5,7},{6,4},{7,5},{8,10},{9,11},{10,... | collective-permute-start | bytes 491528 | tf_op jit(solution)/shard_map/ppermute | solution.py:213
  25.4 7.3 %collective-permute-start.6 = (f32[2,5,8,512]{3,2,1,0:T(8,128)S(1)}, f32[2,5,8,512]{3,2,1,0:T(8,128)S(1)}, u32[]{:S(2)}, u32[]{:S(2)}) collective-permute-start(f32[2,5,8,512]{3,2,1,0:T(8,128)S(1)} %pad_maximum_fusion.3), channel_id=1, source_target_pairs={{0,1},{1,2},{2,3},{3,0},{4,5},{5,6},{6,7},{7,4},{8,9},{9,10},{10,1... | collective-permute-start | bytes 491528 | tf_op jit(solution)/shard_map/ppermute | solution.py:213
  25.7 14.5 %copy-start.9 = (f32[4,8,512]{2,1,0:T(8,128)}, f32[4,8,512]{2,1,0:T(8,128)S(1)}, u32[]{:S(2)}) copy-start(f32[4,8,512]{2,1,0:T(8,128)S(1)} %get-tuple-element.227) | copy-start | bytes 196612
  32.6 7.6 %copy-start.23 = (f32[1,8,512]{2,1,0:T(8,128)}, f32[1,8,512]{2,1,0:T(8,128)S(1)}, u32[]{:S(2)}) copy-start(f32[1,8,512]{2,1,0:T(8,128)S(1)} %get-tuple-element.89) | copy-start | bytes 49156
  32.7 7.6 %copy-start.13 = (f32[1,8,512]{2,1,0:T(8,128)}, f32[1,8,512]{2,1,0:T(8,128)S(1)}, u32[]{:S(2)}) copy-start(f32[1,8,512]{2,1,0:T(8,128)S(1)} %get-tuple-element.86) | copy-start | bytes 49156
  41.0 0.9 copy-start.27
  43.6 33.2 %all-to-all-start = ((f32[64,1,640]{2,1,0:T(1,128)}), f32[64,1,640]{2,1,0:T(1,128)S(1)}, u32[]{:S(2)}, u32[]{:S(2)}) async-start(f32[64,1,640]{2,1,0:T(1,128)} %reshape.257), calls=%async_computation | async-start | bytes 327680 | tf_op jit(solution)/shard_map/all_to_all | solution.py:335
  81.7 16.3 %all-to-all-start.1 = ((f32[64,1,448]{2,1,0:T(1,128)}), f32[64,1,448]{2,1,0:T(1,128)S(1)}, u32[]{:S(2)}, u32[]{:S(2)}) async-start(f32[64,1,448]{2,1,0:T(1,128)} %reshape.259), calls=%async_computation.1 | async-start | bytes 262144 | tf_op jit(solution)/shard_map/all_to_all | solution.py:339
  99.0 1.7 %copy-start.28 = (f32[1,8,512]{2,1,0:T(8,128)S(1)}, f32[1,8,512]{2,1,0:T(8,128)}, u32[]{:S(2)}) copy-start(f32[1,8,512]{2,1,0:T(8,128)} %get-tuple-element.88) | copy-start | bytes 49156
  100.5 2.2 %copy-start.19 = (f32[1,8,512]{2,1,0:T(8,128)}, f32[1,8,512]{2,1,0:T(8,128)S(1)}, u32[]{:S(2)}) copy-start(f32[1,8,512]{2,1,0:T(8,128)S(1)} %squeeze.149) | copy-start | bytes 49156
  100.6 2.1 %copy-start.21 = (f32[1,8,512]{2,1,0:T(8,128)}, f32[1,8,512]{2,1,0:T(8,128)S(1)}, u32[]{:S(2)}) copy-start(f32[1,8,512]{2,1,0:T(8,128)S(1)} %slice.1808) | copy-start | bytes 49156
  101.4 1.4 %copy-start.24 = (f32[1,8,512]{2,1,0:T(8,128)S(1)}, f32[1,8,512]{2,1,0:T(8,128)}, u32[]{:S(2)}) copy-start(f32[1,8,512]{2,1,0:T(8,128)} %copy-done.23) | copy-start | bytes 49156
  109.4 6.2 %copy-start.25 = (f32[8,8,64]{2,1,0:T(8,128)S(1)}, f32[8,8,64]{2,1,0:T(8,128)}, u32[]{:S(2)}) copy-start(f32[8,8,64]{2,1,0:T(8,128)} %get-tuple-element.6) | copy-start | bytes 49156
  110.1 7.8 %collective-permute-start.7 = (f32[4,8,512]{2,1,0:T(8,128)S(1)}, f32[4,8,512]{2,1,0:T(8,128)S(1)}, u32[]{:S(2)}, u32[]{:S(2)}) collective-permute-start(f32[4,8,512]{2,1,0:T(8,128)S(1)} %get-tuple-element.364), channel_id=1, source_target_pairs={{0,3},{1,0},{2,1},{3,2},{4,7},{5,4},{6,5},{7,6},{8,11},{9,8},{10,9... | collective-permute-start | bytes 196616 | tf_op jit(solution)/shard_map/ppermute | solution.py:213
  113.9 4.0 %collective-permute-start.8 = (f32[4,8,512]{2,1,0:T(8,128)S(1)}, f32[4,8,512]{2,1,0:T(8,128)S(1)}, u32[]{:S(2)}, u32[]{:S(2)}) collective-permute-start(f32[4,8,512]{2,1,0:T(8,128)S(1)} %get-tuple-element.364), channel_id=1, source_target_pairs={{0,2},{1,3},{2,0},{3,1},{4,6},{5,7},{6,4},{7,5},{8,10},{9,11},{10,... | collective-permute-start | bytes 196616 | tf_op jit(solution)/shard_map/ppermute | solution.py:213
  113.9 4.0 %collective-permute-start.9 = (f32[4,8,512]{2,1,0:T(8,128)S(1)}, f32[4,8,512]{2,1,0:T(8,128)S(1)}, u32[]{:S(2)}, u32[]{:S(2)}) collective-permute-start(f32[4,8,512]{2,1,0:T(8,128)S(1)} %get-tuple-element.364), channel_id=1, source_target_pairs={{0,1},{1,2},{2,3},{3,0},{4,5},{5,6},{6,7},{7,4},{8,9},{9,10},{10,1... | collective-permute-start | bytes 196616 | tf_op jit(solution)/shard_map/ppermute | solution.py:213
  (30 other events, 21.3 us)

commit v4 on v3

--- a/solution.py
+++ b/solution.py
@@ -221,23 +221,35 @@
     return jnp.concatenate(pieces, axis)
 
 
-def field_halos(fields):
+def field_halos(fields, y_prev, y_next, z_prev, z_next):
     rows = lax.axis_size("row")
     cols = lax.axis_size("col")
     down_rows = [(i, i + 1) for i in range(rows - 1)]
     up_rows = [(i + 1, i) for i in range(rows - 1)]
     down_cols = [(i, i + 1) for i in range(cols - 1)]
     up_cols = [(i + 1, i) for i in range(cols - 1)]
-    from_prev = lax.ppermute(jnp.stack([f[-1:] for f in fields]), "row", down_rows)
-    from_next = lax.ppermute(jnp.stack([f[:1] for f in fields]), "row", up_rows)
-    ext_y = [
-        jnp.concatenate([from_prev[k], f, from_next[k]], 0) for k, f in enumerate(fields)
-    ]
-    from_left = lax.ppermute(jnp.stack([e[:, -1:] for e in ext_y]), "col", down_cols)
-    from_right = lax.ppermute(jnp.stack([e[:, :1] for e in ext_y]), "col", up_cols)
-    return [
-        jnp.concatenate([from_left[k], e, from_right[k]], 1) for k, e in enumerate(ext_y)
-    ]
+
+    def exchange(pieces_of, chosen, pairs, axis):
+        moved = lax.ppermute(jnp.stack([pieces_of[k] for k in chosen]), axis, pairs)
+        return {k: moved[n] for n, k in enumerate(chosen)}
+
+    from_prev = exchange([f[-1:] for f in fields], y_prev, down_rows, "row")
+    from_next = exchange([f[:1] for f in fields], y_next, up_rows, "row")
+    ext_y = []
+    for k, f in enumerate(fields):
+        zero = jnp.zeros_like(f[:1])
+        ext_y.append(
+            jnp.concatenate([from_prev.get(k, zero), f, from_next.get(k, zero)], 0)
+        )
+    from_left = exchange([e[:, -1:] for e in ext_y], z_prev, down_cols, "col")
+    from_right = exchange([e[:, :1] for e in ext_y], z_next, up_cols, "col")
+    ext = []
+    for k, e in enumerate(ext_y):
+        zero = jnp.zeros_like(e[:, :1])
+        ext.append(
+            jnp.concatenate([from_left.get(k, zero), e, from_right.get(k, zero)], 1)
+        )
+    return ext
 
 
 def on_device(
@@ -250,7 +262,11 @@
     col_index = lax.axis_index("col")
 
     ext = field_halos(
-        [efield_x, efield_y, efield_z, hfield_x, hfield_y, hfield_z, permittivity, conductivity]
+        [efield_x, efield_y, efield_z, hfield_x, hfield_y, hfield_z, permittivity, conductivity],
+        y_prev=(1, 2, 3, 5, 6, 7),
+        y_next=(2,),
+        z_prev=(0, 2, 3, 4, 6, 7),
+        z_next=(0,),
     )
     inside = inside_mask(count_y, count_z)
     ex_e, ey_e, ez_e = ext[0], ext[1], ext[2]

time: 124 us -> 119 us (0.960)
  starting transfers between devices: 46.8 us -> 42.6 us
    all_to_all x1, starting transfers between devices: 21.1 us -> 18.1 us  [on_device(): lax.all_to_all(payload, 'row', split_axis=0, concat_axis=0, tiled=True)]
    ppermute x4, starting transfers between devices: 12.9 us -> 11.6 us  [exchange(): moved = lax.ppermute(jnp.stack([pieces_of[k] for k in chosen]), axis, pairs)]
    unnamed x104 -> x99, local copies, waits for them, and re-layouts: 15.1 us -> 15 us
  transfers between devices with their start and end apart: 12 -> 12, of which waited for: 4 -> 3; matrix products, arithmetic and copies ran while one was open for 9% -> 9% of each run, Pallas kernels for 0% -> 0%
where the time goes in v4:
time: 119 us; the launch traced here: 118 us
  starting transfers between devices  42.6 us (36%)
  local copies, waits for them, and re-layouts  27.4 us (23%)
  waiting for transfers between devices  24.4 us (21%)
  other arithmetic  20.9 us (18%)
  between operations  2.93 us (2%)
    all_to_all x1, starting transfers between devices, on_device(): lax.all_to_all(payload, 'row', split_axis=0, concat_axis=0, tiled=True)  18.1 us
    unnamed x99, local copies, waits for them, and re-layouts  15 us
    all_to_all x1, waiting for transfers between devices, on_device(): lax.all_to_all(answer, 'row', split_axis=0, concat_axis=0, tiled=True)  11.7 us
    ppermute x4, starting transfers between devices, exchange(): moved = lax.ppermute(jnp.stack([pieces_of[k] for k in chosen]), axis, pairs)  11.6 us
    all_to_all x1, waiting for transfers between devices, on_device(): lax.all_to_all(payload, 'row', split_axis=0, concat_axis=0, tiled=True)  11.4 us
    ppermute x6, starting transfers between devices, gather_cols(): lax.ppermute(block, 'col', [(i, (i + shift) % cols) for i in range(cols)])  8.25 us
    sub x30, other arithmetic, reduce_lines(): source = source - src_lo * ratio_lo - src_hi * ratio_hi  5.77 us
    all_to_all x1, starting transfers between devices, on_device(): lax.all_to_all(answer, 'row', split_axis=0, concat_axis=0, tiled=True)  4.62 us
  transfers between devices with their start and end apart: 12, of which 3 were waited for; matrix products, arithmetic and copies ran while one was open for 9% of the time, Pallas kernels for 0%

profile of v4, /device:TPU:1, one launch (start us, length us, event | category | flops | bytes accessed | tf_op | source)
XLA Modules:
  0.0 118.2 jit_solution(5548031890210730451)
XLA Ops:
  0.6 0.8 constant_dynamic-update-slice_fusion.5
  2.1 0.8 constant_dynamic-update-slice_fusion.3
  2.9 0.8 constant_dynamic-update-slice_fusion.1
  4.3 3.9 %collective-permute-start = (f32[6,1,8,512]{3,2,1,0:T(8,128)S(1)}, f32[6,1,8,512]{3,2,1,0:T(8,128)S(1)}, u32[]{:S(2)}, u32[]{:S(2)}) collective-permute-start(f32[6,1,8,512]{3,2,1,0:T(8,128)S(1)} %constant_dynamic-update-slice_fusion), channel_id=1, source_target_pairs={{0,4},{4,8},{8,12},{12,16},{16,20},{20,24},{24,28},{28,32},{32,36}... | collective-permute-start | bytes 294920 | tf_op jit(solution)/shard_map/ppermute | solution.py:233
  8.3 1.3 %collective-permute-start.1 = (f32[1,1,8,512]{3,2,1,0:T(8,128)S(1)}, f32[1,1,8,512]{3,2,1,0:T(8,128)S(1)}, u32[]{:S(2)}, u32[]{:S(2)}) collective-permute-start(f32[1,1,8,512]{3,2,1,0:T(8,128)S(1)} %slice_bitcast_fusion.8), channel_id=1, source_target_pairs={{4,0},{8,4},{12,8},{16,12},{20,16},{24,20},{28,24},{32,28},{36,32}... | collective-permute-start | bytes 49160 | tf_op jit(solution)/shard_map/ppermute | solution.py:233
  9.6 2.9 %collective-permute-start.3 = (f32[1,6,1,512]{3,2,1,0:T(1,128)S(1)}, f32[1,6,1,512]{3,2,1,0:T(1,128)S(1)}, u32[]{:S(2)}, u32[]{:S(2)}) collective-permute-start(f32[1,6,1,512]{3,2,1,0:T(1,128)S(1)} %maximum_bitcast_fusion), channel_id=1, source_target_pairs={{1,0},{2,1},{3,2},{5,4},{6,5},{7,6},{9,8},{10,9},{11,10},{13,12},{... | collective-permute-start | bytes 36872 | tf_op jit(solution)/shard_map/ppermute | solution.py:233
  14.8 0.8 copy-done.3
  15.7 0.8 copy-done.10
  16.6 3.5 %collective-permute-start.2 = (f32[6,6,1,512]{3,2,1,0:T(1,128)S(1)}, f32[6,6,1,512]{3,2,1,0:T(1,128)S(1)}, u32[]{:S(2)}, u32[]{:S(2)}) collective-permute-start(f32[6,6,1,512]{3,2,1,0:T(1,128)S(1)} %constant_dynamic-update-slice_fusion.6), channel_id=1, source_target_pairs={{0,1},{1,2},{2,3},{4,5},{5,6},{6,7},{8,9},{9,10},{10,11},{12,13},{... | collective-permute-start | bytes 221192 | tf_op jit(solution)/shard_map/ppermute | solution.py:233
  20.2 1.3 %collective-permute-done.2 = f32[6,6,1,512]{3,2,1,0:T(1,128)S(1)} collective-permute-done((f32[6,6,1,512]{3,2,1,0:T(1,128)S(1)}, f32[6,6,1,512]{3,2,1,0:T(1,128)S(1)}, u32[]{:S(2)}, u32[]{:S(2)}) %collective-permute-start.2) | collective-permute-done | bytes 73760 | tf_op jit(solution)/shard_map/ppermute | solution.py:233
  22.0 2.5 %collective-permute-start.5 = (f32[2,5,8,512]{3,2,1,0:T(8,128)S(1)}, f32[2,5,8,512]{3,2,1,0:T(8,128)S(1)}, u32[]{:S(2)}, u32[]{:S(2)}) collective-permute-start(f32[2,5,8,512]{3,2,1,0:T(8,128)S(1)} %pad_maximum_fusion.7), channel_id=1, source_target_pairs={{0,2},{1,3},{2,0},{3,1},{4,6},{5,7},{6,4},{7,5},{8,10},{9,11},{10,... | collective-permute-start | bytes 491528 | tf_op jit(solution)/shard_map/ppermute | solution.py:213
  41.1 1.0 reshape.258
  42.1 18.1 %all-to-all-start = ((f32[64,1,640]{2,1,0:T(1,128)}), f32[64,1,640]{2,1,0:T(1,128)S(1)}, u32[]{:S(2)}, u32[]{:S(2)}) async-start(f32[64,1,640]{2,1,0:T(1,128)} %reshape.258), calls=%async_computation | async-start | bytes 327680 | tf_op jit(solution)/shard_map/all_to_all | solution.py:351
  61.0 11.4 %all-to-all-done = f32[64,1,640]{2,1,0:T(1,128)S(1)} async-done(((f32[64,1,640]{2,1,0:T(1,128)}), f32[64,1,640]{2,1,0:T(1,128)S(1)}, u32[]{:S(2)}, u32[]{:S(2)}) %all-to-all-start) | async-done | bytes 163872 | tf_op jit(solution)/shard_map/all_to_all | solution.py:351
  72.9 1.0 reduce.28
  76.5 0.8 reshape.260
  77.3 4.6 %all-to-all-start.1 = ((f32[64,1,448]{2,1,0:T(1,128)}), f32[64,1,448]{2,1,0:T(1,128)S(1)}, u32[]{:S(2)}, u32[]{:S(2)}) async-start(f32[64,1,448]{2,1,0:T(1,128)} %reshape.260), calls=%async_computation.1 | async-start | bytes 262144 | tf_op jit(solution)/shard_map/all_to_all | solution.py:355
  82.0 11.7 %all-to-all-done.1 = f32[64,1,448]{2,1,0:T(1,128)S(1)} async-done(((f32[64,1,448]{2,1,0:T(1,128)}), f32[64,1,448]{2,1,0:T(1,128)S(1)}, u32[]{:S(2)}, u32[]{:S(2)}) %all-to-all-start.1) | async-done | bytes 114720 | tf_op jit(solution)/shard_map/all_to_all | solution.py:355
  93.6 1.0 reduce.29
  94.7 1.1 slice_reduce_fusion
  97.0 1.4 %constant_dynamic-update-slice_fusion.29 = (f32[5,8,512]{2,1,0:T(8,128)S(1)}, f32[1,8,512]{2,1,0:T(8,128)S(1)}, f32[1,8,512]{2,1,0:T(8,128)}) fusion(f32[5,8,512]{2,1,0:T(8,128)S(1)} %constant_dynamic-update-slice_fusion.30, f32[1,8,512]{2,1,0:T(8,128)S(1)} %squeeze.49, f32[1,8,512]{2,1,0:T(8,128)S(1)} %copy-done.13, ...), kind=kLoop, calls=%fused_computation.221 | loop fusion | flops 65536 | bytes 245760
  105.8 3.8 %collective-permute-start.7 = (f32[4,8,512]{2,1,0:T(8,128)S(1)}, f32[4,8,512]{2,1,0:T(8,128)S(1)}, u32[]{:S(2)}, u32[]{:S(2)}) collective-permute-start(f32[4,8,512]{2,1,0:T(8,128)S(1)} %get-tuple-element.330), channel_id=1, source_target_pairs={{0,3},{1,0},{2,1},{3,2},{4,7},{5,4},{6,5},{7,6},{8,11},{9,8},{10,9... | collective-permute-start | bytes 196616 | tf_op jit(solution)/shard_map/ppermute | solution.py:213
  109.6 1.6 %collective-permute-start.9 = (f32[4,8,512]{2,1,0:T(8,128)S(1)}, f32[4,8,512]{2,1,0:T(8,128)S(1)}, u32[]{:S(2)}, u32[]{:S(2)}) collective-permute-start(f32[4,8,512]{2,1,0:T(8,128)S(1)} %get-tuple-element.330), channel_id=1, source_target_pairs={{0,1},{1,2},{2,3},{3,0},{4,5},{5,6},{6,7},{7,4},{8,9},{9,10},{10,1... | collective-permute-start | bytes 196616 | tf_op jit(solution)/shard_map/ppermute | solution.py:213
  112.0 1.6 %fusion.55 = (f32[4,8,512]{2,1,0:T(8,128)}, f32[4,8,512]{2,1,0:T(8,128)}) fusion(f32[1,8,512]{2,1,0:T(8,128)S(1)} %slice.1684, f32[1,8,512]{2,1,0:T(8,128)S(1)} %copy-done.19, f32[1,8,512]{2,1,0:T(8,128)S(1)} %get-tuple-element.448, f32[1,8,512]{2,1,0:T(8,128)S(1)} %copy-done.28, f32[5,9,512]{2,1,0:T(8,128)} %copy-done.2, ...), kind=kLoop, calls=%fused_computation.265 | loop fusion | flops 163840 | bytes 344064 | tf_op jit(solution)/shard_map/add | solution.py:389
  (410 shorter events, 37.0 us)
Async XLA Ops:
  0.6 2.2 %copy-start.1 = (f32[4,8,512]{2,1,0:T(8,128)S(1)}, f32[4,8,512]{2,1,0:T(8,128)}, u32[]{:S(2)}) copy-start(f32[4,8,512]{2,1,0:T(8,128)} %param.13) | copy-start | bytes 196612
  2.1 6.2 %copy-start.6 = (f32[4,8,512]{2,1,0:T(8,128)S(1)}, f32[4,8,512]{2,1,0:T(8,128)}, u32[]{:S(2)}) copy-start(f32[4,8,512]{2,1,0:T(8,128)} %param.10) | copy-start | bytes 196612
  2.9 6.7 %copy-start = (f32[4,8,512]{2,1,0:T(8,128)S(1)}, f32[4,8,512]{2,1,0:T(8,128)}, u32[]{:S(2)}) copy-start(f32[4,8,512]{2,1,0:T(8,128)} %param.8) | copy-start | bytes 196612
  4.3 10.4 %collective-permute-start = (f32[6,1,8,512]{3,2,1,0:T(8,128)S(1)}, f32[6,1,8,512]{3,2,1,0:T(8,128)S(1)}, u32[]{:S(2)}, u32[]{:S(2)}) collective-permute-start(f32[6,1,8,512]{3,2,1,0:T(8,128)S(1)} %constant_dynamic-update-slice_fusion), channel_id=1, source_target_pairs={{0,4},{4,8},{8,12},{12,16},{16,20},{20,24},{24,28},{28,32},{32,36}... | collective-permute-start | bytes 294920 | tf_op jit(solution)/shard_map/ppermute | solution.py:233
  8.3 6.5 %collective-permute-start.1 = (f32[1,1,8,512]{3,2,1,0:T(8,128)S(1)}, f32[1,1,8,512]{3,2,1,0:T(8,128)S(1)}, u32[]{:S(2)}, u32[]{:S(2)}) collective-permute-start(f32[1,1,8,512]{3,2,1,0:T(8,128)S(1)} %slice_bitcast_fusion.8), channel_id=1, source_target_pairs={{4,0},{8,4},{12,8},{16,12},{20,16},{24,20},{28,24},{32,28},{36,32}... | collective-permute-start | bytes 49160 | tf_op jit(solution)/shard_map/ppermute | solution.py:233
  9.6 15.3 %collective-permute-start.3 = (f32[1,6,1,512]{3,2,1,0:T(1,128)S(1)}, f32[1,6,1,512]{3,2,1,0:T(1,128)S(1)}, u32[]{:S(2)}, u32[]{:S(2)}) collective-permute-start(f32[1,6,1,512]{3,2,1,0:T(1,128)S(1)} %maximum_bitcast_fusion), channel_id=1, source_target_pairs={{1,0},{2,1},{3,2},{5,4},{6,5},{7,6},{9,8},{10,9},{11,10},{13,12},{... | collective-permute-start | bytes 36872 | tf_op jit(solution)/shard_map/ppermute | solution.py:233
  13.4 11.9 %copy-start.36 = (pred[512]{0:T(512)(128)(4,1)}, pred[512]{0:T(512)(128)(4,1)S(1)}, u32[]{:S(2)}) copy-start(pred[512]{0:T(512)(128)(4,1)S(1)} %get-tuple-element.463) | copy-start | bytes 1540
  13.4 12.4 %copy-start.32 = (pred[512]{0:T(512)(128)(4,1)}, pred[512]{0:T(512)(128)(4,1)S(1)}, u32[]{:S(2)}) copy-start(pred[512]{0:T(512)(128)(4,1)S(1)} %get-tuple-element.464) | copy-start | bytes 1540
  16.5 3.6 %copy-start.11 = (f32[4,8,512]{2,1,0:T(8,128)S(1)}, f32[4,8,512]{2,1,0:T(8,128)}, u32[]{:S(2)}) copy-start(f32[4,8,512]{2,1,0:T(8,128)} %param.9) | copy-start | bytes 196612
  16.6 4.9 %collective-permute-start.2 = (f32[6,6,1,512]{3,2,1,0:T(1,128)S(1)}, f32[6,6,1,512]{3,2,1,0:T(1,128)S(1)}, u32[]{:S(2)}, u32[]{:S(2)}) collective-permute-start(f32[6,6,1,512]{3,2,1,0:T(1,128)S(1)} %constant_dynamic-update-slice_fusion.6), channel_id=1, source_target_pairs={{0,1},{1,2},{2,3},{4,5},{5,6},{6,7},{8,9},{9,10},{10,11},{12,13},{... | collective-permute-start | bytes 221192 | tf_op jit(solution)/shard_map/ppermute | solution.py:233
  22.0 9.9 %collective-permute-start.4 = (f32[2,5,8,512]{3,2,1,0:T(8,128)S(1)}, f32[2,5,8,512]{3,2,1,0:T(8,128)S(1)}, u32[]{:S(2)}, u32[]{:S(2)}) collective-permute-start(f32[2,5,8,512]{3,2,1,0:T(8,128)S(1)} %pad_maximum_fusion.7), channel_id=1, source_target_pairs={{0,3},{1,0},{2,1},{3,2},{4,7},{5,4},{6,5},{7,6},{8,11},{9,8},{10,9... | collective-permute-start | bytes 491528 | tf_op jit(solution)/shard_map/ppermute | solution.py:213
  22.0 9.8 %collective-permute-start.5 = (f32[2,5,8,512]{3,2,1,0:T(8,128)S(1)}, f32[2,5,8,512]{3,2,1,0:T(8,128)S(1)}, u32[]{:S(2)}, u32[]{:S(2)}) collective-permute-start(f32[2,5,8,512]{3,2,1,0:T(8,128)S(1)} %pad_maximum_fusion.7), channel_id=1, source_target_pairs={{0,2},{1,3},{2,0},{3,1},{4,6},{5,7},{6,4},{7,5},{8,10},{9,11},{10,... | collective-permute-start | bytes 491528 | tf_op jit(solution)/shard_map/ppermute | solution.py:213
  24.5 7.3 %collective-permute-start.6 = (f32[2,5,8,512]{3,2,1,0:T(8,128)S(1)}, f32[2,5,8,512]{3,2,1,0:T(8,128)S(1)}, u32[]{:S(2)}, u32[]{:S(2)}) collective-permute-start(f32[2,5,8,512]{3,2,1,0:T(8,128)S(1)} %pad_maximum_fusion.7), channel_id=1, source_target_pairs={{0,1},{1,2},{2,3},{3,0},{4,5},{5,6},{6,7},{7,4},{8,9},{9,10},{10,1... | collective-permute-start | bytes 491528 | tf_op jit(solution)/shard_map/ppermute | solution.py:213
  31.8 7.0 %copy-start.22 = (f32[1,8,512]{2,1,0:T(8,128)}, f32[1,8,512]{2,1,0:T(8,128)S(1)}, u32[]{:S(2)}) copy-start(f32[1,8,512]{2,1,0:T(8,128)S(1)} %get-tuple-element.89) | copy-start | bytes 49156
  31.8 7.0 %copy-start.12 = (f32[1,8,512]{2,1,0:T(8,128)}, f32[1,8,512]{2,1,0:T(8,128)S(1)}, u32[]{:S(2)}) copy-start(f32[1,8,512]{2,1,0:T(8,128)S(1)} %get-tuple-element.86) | copy-start | bytes 49156
  42.1 30.3 %all-to-all-start = ((f32[64,1,640]{2,1,0:T(1,128)}), f32[64,1,640]{2,1,0:T(1,128)S(1)}, u32[]{:S(2)}, u32[]{:S(2)}) async-start(f32[64,1,640]{2,1,0:T(1,128)} %reshape.258), calls=%async_computation | async-start | bytes 327680 | tf_op jit(solution)/shard_map/all_to_all | solution.py:351
  77.3 16.3 %all-to-all-start.1 = ((f32[64,1,448]{2,1,0:T(1,128)}), f32[64,1,448]{2,1,0:T(1,128)S(1)}, u32[]{:S(2)}, u32[]{:S(2)}) async-start(f32[64,1,448]{2,1,0:T(1,128)} %reshape.260), calls=%async_computation.1 | async-start | bytes 262144 | tf_op jit(solution)/shard_map/all_to_all | solution.py:355
  94.6 1.7 %copy-start.27 = (f32[1,8,512]{2,1,0:T(8,128)S(1)}, f32[1,8,512]{2,1,0:T(8,128)}, u32[]{:S(2)}) copy-start(f32[1,8,512]{2,1,0:T(8,128)} %get-tuple-element.88) | copy-start | bytes 49156
  96.1 2.2 %copy-start.18 = (f32[1,8,512]{2,1,0:T(8,128)}, f32[1,8,512]{2,1,0:T(8,128)S(1)}, u32[]{:S(2)}) copy-start(f32[1,8,512]{2,1,0:T(8,128)S(1)} %squeeze.50) | copy-start | bytes 49156
  96.2 2.1 %copy-start.20 = (f32[1,8,512]{2,1,0:T(8,128)}, f32[1,8,512]{2,1,0:T(8,128)S(1)}, u32[]{:S(2)}) copy-start(f32[1,8,512]{2,1,0:T(8,128)S(1)} %slice.1681) | copy-start | bytes 49156
  105.1 6.2 %copy-start.24 = (f32[8,8,64]{2,1,0:T(8,128)S(1)}, f32[8,8,64]{2,1,0:T(8,128)}, u32[]{:S(2)}) copy-start(f32[8,8,64]{2,1,0:T(8,128)} %get-tuple-element.6) | copy-start | bytes 49156
  105.8 7.8 %collective-permute-start.7 = (f32[4,8,512]{2,1,0:T(8,128)S(1)}, f32[4,8,512]{2,1,0:T(8,128)S(1)}, u32[]{:S(2)}, u32[]{:S(2)}) collective-permute-start(f32[4,8,512]{2,1,0:T(8,128)S(1)} %get-tuple-element.330), channel_id=1, source_target_pairs={{0,3},{1,0},{2,1},{3,2},{4,7},{5,4},{6,5},{7,6},{8,11},{9,8},{10,9... | collective-permute-start | bytes 196616 | tf_op jit(solution)/shard_map/ppermute | solution.py:213
  109.6 4.0 %collective-permute-start.8 = (f32[4,8,512]{2,1,0:T(8,128)S(1)}, f32[4,8,512]{2,1,0:T(8,128)S(1)}, u32[]{:S(2)}, u32[]{:S(2)}) collective-permute-start(f32[4,8,512]{2,1,0:T(8,128)S(1)} %get-tuple-element.330), channel_id=1, source_target_pairs={{0,2},{1,3},{2,0},{3,1},{4,6},{5,7},{6,4},{7,5},{8,10},{9,11},{10,... | collective-permute-start | bytes 196616 | tf_op jit(solution)/shard_map/ppermute | solution.py:213
  109.6 4.0 %collective-permute-start.9 = (f32[4,8,512]{2,1,0:T(8,128)S(1)}, f32[4,8,512]{2,1,0:T(8,128)S(1)}, u32[]{:S(2)}, u32[]{:S(2)}) collective-permute-start(f32[4,8,512]{2,1,0:T(8,128)S(1)} %get-tuple-element.330), channel_id=1, source_target_pairs={{0,1},{1,2},{2,3},{3,0},{4,5},{5,6},{6,7},{7,4},{8,9},{9,10},{10,1... | collective-permute-start | bytes 196616 | tf_op jit(solution)/shard_map/ppermute | solution.py:213
  (28 other events, 20.4 us)

commit v5 on v4

--- a/solution.py
+++ b/solution.py
@@ -1,9 +1,14 @@
+import functools
+
 import jax
 import jax.numpy as jnp
 from jax import lax
 from jax.sharding import PartitionSpec as P
+from jax.experimental import pallas as pl
+from jax.experimental.pallas import tpu as pltpu
 
 HALF_STEP = 30.0
+INTERPRET = False
 
 
 def with_halo(cells, sides, width):
@@ -83,6 +88,54 @@
     is_first, is_final = line_flags(source.shape[line_axis], line_axis, source.ndim)
     sub_diag, main_diag, super_diag = line_system(coupling, is_first, is_final)
     return reduce_lines(sub_diag, main_diag, super_diag, source, line_axis)
+
+
+def _line_solve_kernel(source_ref, coupling_ref, out_ref, *, line_axis):
+    source = source_ref[...]
+    coupling = coupling_ref[...]
+    length = source.shape[line_axis]
+    where_line = lax.broadcasted_iota(jnp.int32, source.shape, line_axis)
+    is_first = where_line == 0
+    is_final = where_line == length - 1
+    sub_diag = jnp.where(is_first, 0.0, -coupling)
+    main_diag = jnp.where(is_first, 1.0 + coupling, 1.0 + 2.0 * coupling)
+    super_diag = jnp.where(is_final, 0.0, -coupling)
+    stride = 1
+    while stride < length:
+        has_lo = where_line >= stride
+        has_hi = where_line < length - stride
+
+        def lo(values, filler):
+            return jnp.where(has_lo, pltpu.roll(values, stride, line_axis), filler)
+
+        def hi(values, filler):
+            return jnp.where(has_hi, pltpu.roll(values, length - stride, line_axis), filler)
+
+        sub_lo = lo(sub_diag, 0.0)
+        mid_lo = lo(main_diag, 1.0)
+        sup_lo = lo(super_diag, 0.0)
+        src_lo = lo(source, 0.0)
+        sub_hi = hi(sub_diag, 0.0)
+        mid_hi = hi(main_diag, 1.0)
+        sup_hi = hi(super_diag, 0.0)
+        src_hi = hi(source, 0.0)
+        ratio_lo = sub_diag / mid_lo
+        ratio_hi = super_diag / mid_hi
+        sub_diag = -sub_lo * ratio_lo
+        super_diag = -sup_hi * ratio_hi
+        main_diag = main_diag - sup_lo * ratio_lo - sub_hi * ratio_hi
+        source = source - src_lo * ratio_lo - src_hi * ratio_hi
+        stride = stride * 2
+    out_ref[...] = source / main_diag
+
+
+def solve_lines(source, coupling, line_axis):
+    kernel = functools.partial(_line_solve_kernel, line_axis=line_axis)
+    return pl.pallas_call(
+        kernel,
+        out_shape=jax.ShapeDtypeStruct(source.shape, source.dtype),
+        interpret=INTERPRET,
+    )(source, coupling)
 
 
 def inside_mask(count_y, count_z):
@@ -307,7 +360,7 @@
 
     gathered = gather_cols(jnp.stack([source_y, coup_e[ya, zs]]), 2)
     coup_full = gathered[1]
-    half_ey_full = solve_local(gathered[0], coup_full, 1)
+    half_ey_full = solve_lines(gathered[0], coup_full, 1)
     pos_y = (
         lax.axis_index("row") * count_y
         + lax.broadcasted_iota(jnp.int32, (count_y + 1, 1, 1), 0)
@@ -317,7 +370,7 @@
     padded = jnp.pad(half_ey_full, ((0, 0), (1, 1), (0, 0)))
     half_ey_e = lax.dynamic_slice_in_dim(padded, col_index * count_z, count_z + 2, axis=1)
 
-    half_ez_e = solve_local(source_z, coup_e[ys, za], 2)
+    half_ez_e = solve_lines(source_z, coup_e[ys, za], 2)
     half_ez_e = jnp.where(inside[ys, za], half_ez_e, 0.0)
 
     half_hy_e = hy_e[ys, za] + HALF_STEP * (diff_up(half_ez_e, 2) - dpz_ex)
@@ -379,12 +432,12 @@
     )
 
     second_full = gather_cols(second_x, 1)
-    next_ex_full = solve_local(second_full, coup_full[1:], 1)
+    next_ex_full = solve_lines(second_full, coup_full[1:], 1)
     padded = jnp.pad(next_ex_full, ((0, 0), (0, 1), (0, 0)))
     next_ex_e = lax.dynamic_slice_in_dim(padded, col_index * count_z, count_z + 1, axis=1)
     next_ex = next_ex_e[:, :-1]
 
-    next_ey = solve_local(second_y, coupling, 2)
+    next_ey = solve_lines(second_y, coupling, 2)
 
     next_hx = half_hx_e[1:, 1:] + HALF_STEP * (
         dz_ey_own[1:] - (next_ez_e[1:] - next_ez_e[:-1])

time: 119 us -> 117 us (0.983)
  local copies, waits for them, and re-layouts: 27.4 us -> 12.7 us
  Pallas kernels: 0 us -> 12.2 us
  other arithmetic: 20.9 us -> 13.4 us
  starting transfers between devices: 42.6 us -> 47.9 us
  waiting for transfers between devices: 24.4 us -> 28.4 us
  between operations: 2.93 us -> 1.69 us
    pallas_call x0 -> x4, Pallas kernels: none -> 12.2 us  [solve_lines(): pl.pallas_call(kernel, out_shape=jax.ShapeDtypeStruct(source.shape, sourc...]
    unnamed x99 -> x39, local copies, waits for them, and re-layouts: 15 us -> 6.77 us
    sub x30 -> x6, other arithmetic: 5.77 us -> 0.26 us  [reduce_lines(): source = source - src_lo * ratio_lo - src_hi * ratio_hi]
    all_to_all x1, starting transfers between devices: 18.1 us -> 22.4 us  [on_device(): lax.all_to_all(payload, 'row', split_axis=0, concat_axis=0, tiled=True)]
    slice x79 -> x23, local copies, waits for them, and re-layouts: 3.55 us -> 0.28 us  [shifted(): lax.slice_in_dim(values, 0, length - stride, axis=line_axis)]
    sub x26 -> x6, other arithmetic: 3.54 us -> 0.28 us  [reduce_lines(): main_diag = main_diag - sup_lo * ratio_lo - sub_hi * ratio_hi]
    ppermute x6, waiting for transfers between devices: 0.02 us -> 3.01 us  [gather_cols(): lax.ppermute(block, 'col', [(i, (i + shift) % cols) for i in range(cols)])]
    slice x66 -> x10, local copies, waits for them, and re-layouts: 3.64 us -> 1.15 us  [shifted(): lax.slice_in_dim(values, stride, length, axis=line_axis)]
  transfers between devices with their start and end apart: 12 -> 12, of which waited for: 3 -> 6; matrix products, arithmetic and copies ran while one was open for 9% -> 6% of each run, Pallas kernels for 0% -> 3%
where the time goes in v5:
time: 117 us; the launch traced here: 116 us
  starting transfers between devices  47.9 us (41%)
  waiting for transfers between devices  28.4 us (24%)
  other arithmetic  13.4 us (11%)
  local copies, waits for them, and re-layouts  12.7 us (11%)
  Pallas kernels  12.2 us (10%)
  between operations  1.69 us (1%)
    all_to_all x1, starting transfers between devices, on_device(): lax.all_to_all(payload, 'row', split_axis=0, concat_axis=0, tiled=True)  22.4 us
    ppermute x4, starting transfers between devices, exchange(): moved = lax.ppermute(jnp.stack([pieces_of[k] for k in chosen]), axis, pairs)  12.8 us
    pallas_call x4, Pallas kernels, solve_lines(): pl.pallas_call(kernel, out_shape=jax.ShapeDtypeStruct(source.shape, sourc...  12.2 us
    all_to_all x1, waiting for transfers between devices, on_device(): lax.all_to_all(payload, 'row', split_axis=0, concat_axis=0, tiled=True)  12 us
    all_to_all x1, waiting for transfers between devices, on_device(): lax.all_to_all(answer, 'row', split_axis=0, concat_axis=0, tiled=True)  10.7 us
    ppermute x6, starting transfers between devices, gather_cols(): lax.ppermute(block, 'col', [(i, (i + shift) % cols) for i in range(cols)])  8.17 us
    unnamed x39, local copies, waits for them, and re-layouts  6.77 us
    all_to_all x1, starting transfers between devices, on_device(): lax.all_to_all(answer, 'row', split_axis=0, concat_axis=0, tiled=True)  4.62 us
  transfers between devices with their start and end apart: 12, of which 6 were waited for; matrix products, arithmetic and copies ran while one was open for 6% of the time, Pallas kernels for 3%

profile of v5, /device:TPU:1, one launch (start us, length us, event | category | flops | bytes accessed | tf_op | source)
XLA Modules:
  0.0 116.4 jit_solution(835709946501880346)
XLA Ops:
  1.6 5.2 %collective-permute-start.3 = (f32[1,6,1,512]{3,2,1,0:T(1,128)S(1)}, f32[1,6,1,512]{3,2,1,0:T(1,128)S(1)}, u32[]{:S(2)}, u32[]{:S(2)}) collective-permute-start(f32[1,6,1,512]{3,2,1,0:T(1,128)S(1)} %maximum_bitcast_fusion.1), channel_id=1, source_target_pairs={{1,0},{2,1},{3,2},{5,4},{6,5},{7,6},{9,8},{10,9},{11,10},{13,12},{... | collective-permute-start | bytes 36872 | tf_op jit(solution)/shard_map/ppermute | solution.py:286
  6.8 1.3 %collective-permute-start.1 = (f32[1,1,8,512]{3,2,1,0:T(8,128)S(1)}, f32[1,1,8,512]{3,2,1,0:T(8,128)S(1)}, u32[]{:S(2)}, u32[]{:S(2)}) collective-permute-start(f32[1,1,8,512]{3,2,1,0:T(8,128)S(1)} %slice_bitcast_fusion.10), channel_id=1, source_target_pairs={{4,0},{8,4},{12,8},{16,12},{20,16},{24,20},{28,24},{32,28},{36,32}... | collective-permute-start | bytes 49160 | tf_op jit(solution)/shard_map/ppermute | solution.py:286
  9.7 4.0 %collective-permute-start = (f32[6,1,8,512]{3,2,1,0:T(8,128)S(1)}, f32[6,1,8,512]{3,2,1,0:T(8,128)S(1)}, u32[]{:S(2)}, u32[]{:S(2)}) collective-permute-start(f32[6,1,8,512]{3,2,1,0:T(8,128)S(1)} %constant_dynamic-update-slice_fusion), channel_id=1, source_target_pairs={{0,4},{4,8},{8,12},{12,16},{16,20},{20,24},{24,28},{28,32},{32,36}... | collective-permute-start | bytes 294920 | tf_op jit(solution)/shard_map/ppermute | solution.py:286
  14.6 1.5 %collective-permute-done = f32[6,1,8,512]{3,2,1,0:T(8,128)S(1)} collective-permute-done((f32[6,1,8,512]{3,2,1,0:T(8,128)S(1)}, f32[6,1,8,512]{3,2,1,0:T(8,128)S(1)}, u32[]{:S(2)}, u32[]{:S(2)}) %collective-permute-start) | collective-permute-done | bytes 98336 | tf_op jit(solution)/shard_map/ppermute | solution.py:286
  17.9 2.2 %collective-permute-start.2 = (f32[6,6,1,512]{3,2,1,0:T(1,128)S(1)}, f32[6,6,1,512]{3,2,1,0:T(1,128)S(1)}, u32[]{:S(2)}, u32[]{:S(2)}) collective-permute-start(f32[6,6,1,512]{3,2,1,0:T(1,128)S(1)} %constant_dynamic-update-slice_fusion.6), channel_id=1, source_target_pairs={{0,1},{1,2},{2,3},{4,5},{5,6},{6,7},{8,9},{9,10},{10,11},{12,13},{... | collective-permute-start | bytes 221192 | tf_op jit(solution)/shard_map/ppermute | solution.py:286
  20.3 1.3 %collective-permute-done.2 = f32[6,6,1,512]{3,2,1,0:T(1,128)S(1)} collective-permute-done((f32[6,6,1,512]{3,2,1,0:T(1,128)S(1)}, f32[6,6,1,512]{3,2,1,0:T(1,128)S(1)}, u32[]{:S(2)}, u32[]{:S(2)}) %collective-permute-start.2) | collective-permute-done | bytes 73760 | tf_op jit(solution)/shard_map/ppermute | solution.py:286
  22.0 2.4 %collective-permute-start.6 = (f32[2,5,8,512]{3,2,1,0:T(8,128)S(1)}, f32[2,5,8,512]{3,2,1,0:T(8,128)S(1)}, u32[]{:S(2)}, u32[]{:S(2)}) collective-permute-start(f32[2,5,8,512]{3,2,1,0:T(8,128)S(1)} %pad_maximum_fusion.6), channel_id=1, source_target_pairs={{0,1},{1,2},{2,3},{3,0},{4,5},{5,6},{6,7},{7,4},{8,9},{9,10},{10,1... | collective-permute-start | bytes 491528 | tf_op jit(solution)/shard_map/ppermute | solution.py:266
  27.1 3.6 %shard_map.127 = f32[4,9,512]{2,1,0:T(8,128)} custom-call(f32[4,9,512]{2,1,0:T(8,128)} %fusion.16.source_ref, f32[4,9,512]{2,1,0:T(8,128)} %slice.869.coupling_ref), custom_call_target="tpu_custom_call" | custom-call | tf_op jit(solution)/shard_map/pallas_call | solution.py:134
  30.7 1.0 broadcast_select_fusion.1
  33.9 3.2 %shard_map.128 = f32[5,32,512]{2,1,0:T(8,128)} custom-call(f32[5,32,512]{2,1,0:T(8,128)} %get-tuple-element.56.source_ref, f32[5,32,512]{2,1,0:T(8,128)} %get-tuple-element.55.coupling_ref), custom_call_target="tpu_custom_call" | custom-call | tf_op jit(solution)/shard_map/pallas_call | solution.py:134
  37.1 1.1 broadcast_select_fusion
  39.0 1.0 reshape.187
  40.0 22.4 %all-to-all-start = ((f32[64,1,640]{2,1,0:T(1,128)}), f32[64,1,640]{2,1,0:T(1,128)S(1)}, u32[]{:S(2)}, u32[]{:S(2)}) async-start(f32[64,1,640]{2,1,0:T(1,128)} %reshape.187), calls=%async_computation | async-start | bytes 327680 | tf_op jit(solution)/shard_map/all_to_all | solution.py:404
  62.4 12.0 %all-to-all-done = f32[64,1,640]{2,1,0:T(1,128)S(1)} async-done(((f32[64,1,640]{2,1,0:T(1,128)}), f32[64,1,640]{2,1,0:T(1,128)S(1)}, u32[]{:S(2)}, u32[]{:S(2)}) %all-to-all-start) | async-done | bytes 163872 | tf_op jit(solution)/shard_map/all_to_all | solution.py:404
  74.9 1.0 reduce
  79.3 4.6 %all-to-all-start.1 = ((f32[64,1,448]{2,1,0:T(1,128)}), f32[64,1,448]{2,1,0:T(1,128)S(1)}, u32[]{:S(2)}, u32[]{:S(2)}) async-start(f32[64,1,448]{2,1,0:T(1,128)} %reshape.189), calls=%async_computation.1 | async-start | bytes 262144 | tf_op jit(solution)/shard_map/all_to_all | solution.py:408
  84.6 10.7 %all-to-all-done.1 = f32[64,1,448]{2,1,0:T(1,128)S(1)} async-done(((f32[64,1,448]{2,1,0:T(1,128)}), f32[64,1,448]{2,1,0:T(1,128)S(1)}, u32[]{:S(2)}, u32[]{:S(2)}) %all-to-all-start.1) | async-done | bytes 114720 | tf_op jit(solution)/shard_map/all_to_all | solution.py:408
  97.8 2.6 %shard_map.130 = f32[4,8,512]{2,1,0:T(8,128)} custom-call(f32[4,8,512]{2,1,0:T(8,128)} %fusion.36.source_ref, f32[4,8,512]{2,1,0:T(8,128)} %get-tuple-element.79.coupling_ref), custom_call_target="tpu_custom_call" | custom-call | tf_op jit(solution)/shard_map/pallas_call | solution.py:134
  100.5 1.0 slice.978
  102.2 3.5 %collective-permute-start.9 = (f32[4,8,512]{2,1,0:T(8,128)S(1)}, f32[4,8,512]{2,1,0:T(8,128)S(1)}, u32[]{:S(2)}, u32[]{:S(2)}) collective-permute-start(f32[4,8,512]{2,1,0:T(8,128)S(1)} %get-tuple-element.108), channel_id=1, source_target_pairs={{0,1},{1,2},{2,3},{3,0},{4,5},{5,6},{6,7},{7,4},{8,9},{9,10},{10,1... | collective-permute-start | bytes 196616 | tf_op jit(solution)/shard_map/ppermute | solution.py:266
  105.7 1.7 %collective-permute-start.8 = (f32[4,8,512]{2,1,0:T(8,128)S(1)}, f32[4,8,512]{2,1,0:T(8,128)S(1)}, u32[]{:S(2)}, u32[]{:S(2)}) collective-permute-start(f32[4,8,512]{2,1,0:T(8,128)S(1)} %get-tuple-element.108), channel_id=1, source_target_pairs={{0,2},{1,3},{2,0},{3,1},{4,6},{5,7},{6,4},{7,5},{8,10},{9,11},{10,... | collective-permute-start | bytes 196616 | tf_op jit(solution)/shard_map/ppermute | solution.py:266
  108.1 2.5 %collective-permute-done.8 = f32[4,8,512]{2,1,0:T(8,128)S(1)} collective-permute-done((f32[4,8,512]{2,1,0:T(8,128)S(1)}, f32[4,8,512]{2,1,0:T(8,128)S(1)}, u32[]{:S(2)}, u32[]{:S(2)}) %collective-permute-start.8) | collective-permute-done | bytes 65568 | tf_op jit(solution)/shard_map/ppermute | solution.py:266
  111.9 2.8 %shard_map.129 = f32[4,32,512]{2,1,0:T(8,128)} custom-call(f32[4,32,512]{2,1,0:T(8,128)} %pad_maximum_fusion.5.source_ref, f32[4,32,512]{2,1,0:T(8,128)} %slice_bitcast_fusion.2.coupling_ref), custom_call_target="tpu_custom_call" | custom-call | tf_op jit(solution)/shard_map/pallas_call | solution.py:134
  114.7 1.7 %fusion.34 = (f32[4,8,512]{2,1,0:T(8,128)}, f32[4,8,512]{2,1,0:T(8,128)}) fusion(s32[]{:T(128)S(6)} %add.295, f32[4,32,512]{2,1,0:T(8,128)} %shard_map.129, f32[4,9,512]{2,1,0:T(8,128)S(1)} %get-tuple-element.52, f32[4,9,512]{2,1,0:T(8,128)S(1)} %get-tuple-element.51, s32[]{:T(128)S(6)} %select_n.281), kind=kLoop, calls=%fused_computation.126 | loop fusion | flops 65536 | bytes 524296 | tf_op jit(solution)/shard_map/add | solution.py:445
  (189 shorter events, 20.5 us)
Async XLA Ops:
  0.6 6.2 %copy-start.6 = (f32[4,8,512]{2,1,0:T(8,128)S(1)}, f32[4,8,512]{2,1,0:T(8,128)}, u32[]{:S(2)}) copy-start(f32[4,8,512]{2,1,0:T(8,128)} %param.10) | copy-start | bytes 196612
  0.7 8.2 %copy-start.3 = (f32[4,8,512]{2,1,0:T(8,128)S(1)}, f32[4,8,512]{2,1,0:T(8,128)}, u32[]{:S(2)}) copy-start(f32[4,8,512]{2,1,0:T(8,128)} %param.11) | copy-start | bytes 196612
  1.5 7.3 %copy-start.1 = (f32[4,8,512]{2,1,0:T(8,128)S(1)}, f32[4,8,512]{2,1,0:T(8,128)}, u32[]{:S(2)}) copy-start(f32[4,8,512]{2,1,0:T(8,128)} %param.13) | copy-start | bytes 196612
  1.6 24.7 %collective-permute-start.3 = (f32[1,6,1,512]{3,2,1,0:T(1,128)S(1)}, f32[1,6,1,512]{3,2,1,0:T(1,128)S(1)}, u32[]{:S(2)}, u32[]{:S(2)}) collective-permute-start(f32[1,6,1,512]{3,2,1,0:T(1,128)S(1)} %maximum_bitcast_fusion.1), channel_id=1, source_target_pairs={{1,0},{2,1},{3,2},{5,4},{6,5},{7,6},{9,8},{10,9},{11,10},{13,12},{... | collective-permute-start | bytes 36872 | tf_op jit(solution)/shard_map/ppermute | solution.py:286
  6.8 9.3 %collective-permute-start.1 = (f32[1,1,8,512]{3,2,1,0:T(8,128)S(1)}, f32[1,1,8,512]{3,2,1,0:T(8,128)S(1)}, u32[]{:S(2)}, u32[]{:S(2)}) collective-permute-start(f32[1,1,8,512]{3,2,1,0:T(8,128)S(1)} %slice_bitcast_fusion.10), channel_id=1, source_target_pairs={{4,0},{8,4},{12,8},{16,12},{20,16},{24,20},{28,24},{32,28},{36,32}... | collective-permute-start | bytes 49160 | tf_op jit(solution)/shard_map/ppermute | solution.py:286
  8.8 0.8 copy-start.7
  9.7 6.5 %collective-permute-start = (f32[6,1,8,512]{3,2,1,0:T(8,128)S(1)}, f32[6,1,8,512]{3,2,1,0:T(8,128)S(1)}, u32[]{:S(2)}, u32[]{:S(2)}) collective-permute-start(f32[6,1,8,512]{3,2,1,0:T(8,128)S(1)} %constant_dynamic-update-slice_fusion), channel_id=1, source_target_pairs={{0,4},{4,8},{8,12},{12,16},{16,20},{20,24},{24,28},{28,32},{32,36}... | collective-permute-start | bytes 294920 | tf_op jit(solution)/shard_map/ppermute | solution.py:286
  13.7 0.8 copy-start
  16.2 0.8 copy-start.4
  17.0 0.8 copy-start.8
  17.9 2.3 %copy-start.9 = (f32[4,8,512]{2,1,0:T(8,128)S(1)}, f32[4,8,512]{2,1,0:T(8,128)}, u32[]{:S(2)}) copy-start(f32[4,8,512]{2,1,0:T(8,128)} %param.9) | copy-start | bytes 196612
  17.9 3.6 %collective-permute-start.2 = (f32[6,6,1,512]{3,2,1,0:T(1,128)S(1)}, f32[6,6,1,512]{3,2,1,0:T(1,128)S(1)}, u32[]{:S(2)}, u32[]{:S(2)}) collective-permute-start(f32[6,6,1,512]{3,2,1,0:T(1,128)S(1)} %constant_dynamic-update-slice_fusion.6), channel_id=1, source_target_pairs={{0,1},{1,2},{2,3},{4,5},{5,6},{6,7},{8,9},{9,10},{10,11},{12,13},{... | collective-permute-start | bytes 221192 | tf_op jit(solution)/shard_map/ppermute | solution.py:286
  22.0 10.8 %collective-permute-start.6 = (f32[2,5,8,512]{3,2,1,0:T(8,128)S(1)}, f32[2,5,8,512]{3,2,1,0:T(8,128)S(1)}, u32[]{:S(2)}, u32[]{:S(2)}) collective-permute-start(f32[2,5,8,512]{3,2,1,0:T(8,128)S(1)} %pad_maximum_fusion.6), channel_id=1, source_target_pairs={{0,1},{1,2},{2,3},{3,0},{4,5},{5,6},{6,7},{7,4},{8,9},{9,10},{10,1... | collective-permute-start | bytes 491528 | tf_op jit(solution)/shard_map/ppermute | solution.py:266
  24.5 8.3 %collective-permute-start.5 = (f32[2,5,8,512]{3,2,1,0:T(8,128)S(1)}, f32[2,5,8,512]{3,2,1,0:T(8,128)S(1)}, u32[]{:S(2)}, u32[]{:S(2)}) collective-permute-start(f32[2,5,8,512]{3,2,1,0:T(8,128)S(1)} %pad_maximum_fusion.6), channel_id=1, source_target_pairs={{0,2},{1,3},{2,0},{3,1},{4,6},{5,7},{6,4},{7,5},{8,10},{9,11},{10,... | collective-permute-start | bytes 491528 | tf_op jit(solution)/shard_map/ppermute | solution.py:266
  24.5 8.3 %collective-permute-start.4 = (f32[2,5,8,512]{3,2,1,0:T(8,128)S(1)}, f32[2,5,8,512]{3,2,1,0:T(8,128)S(1)}, u32[]{:S(2)}, u32[]{:S(2)}) collective-permute-start(f32[2,5,8,512]{3,2,1,0:T(8,128)S(1)} %pad_maximum_fusion.6), channel_id=1, source_target_pairs={{0,3},{1,0},{2,1},{3,2},{4,7},{5,4},{6,5},{7,6},{8,11},{9,8},{10,9... | collective-permute-start | bytes 491528 | tf_op jit(solution)/shard_map/ppermute | solution.py:266
  31.7 0.9 copy-start.2
  40.0 34.4 %all-to-all-start = ((f32[64,1,640]{2,1,0:T(1,128)}), f32[64,1,640]{2,1,0:T(1,128)S(1)}, u32[]{:S(2)}, u32[]{:S(2)}) async-start(f32[64,1,640]{2,1,0:T(1,128)} %reshape.187), calls=%async_computation | async-start | bytes 327680 | tf_op jit(solution)/shard_map/all_to_all | solution.py:404
  79.3 16.0 %all-to-all-start.1 = ((f32[64,1,448]{2,1,0:T(1,128)}), f32[64,1,448]{2,1,0:T(1,128)S(1)}, u32[]{:S(2)}, u32[]{:S(2)}) async-start(f32[64,1,448]{2,1,0:T(1,128)} %reshape.189), calls=%async_computation.1 | async-start | bytes 262144 | tf_op jit(solution)/shard_map/all_to_all | solution.py:408
  100.5 1.0 copy-start.5
  102.2 6.0 %collective-permute-start.9 = (f32[4,8,512]{2,1,0:T(8,128)S(1)}, f32[4,8,512]{2,1,0:T(8,128)S(1)}, u32[]{:S(2)}, u32[]{:S(2)}) collective-permute-start(f32[4,8,512]{2,1,0:T(8,128)S(1)} %get-tuple-element.108), channel_id=1, source_target_pairs={{0,1},{1,2},{2,3},{3,0},{4,5},{5,6},{6,7},{7,4},{8,9},{9,10},{10,1... | collective-permute-start | bytes 196616 | tf_op jit(solution)/shard_map/ppermute | solution.py:266
  105.7 4.9 %collective-permute-start.8 = (f32[4,8,512]{2,1,0:T(8,128)S(1)}, f32[4,8,512]{2,1,0:T(8,128)S(1)}, u32[]{:S(2)}, u32[]{:S(2)}) collective-permute-start(f32[4,8,512]{2,1,0:T(8,128)S(1)} %get-tuple-element.108), channel_id=1, source_target_pairs={{0,2},{1,3},{2,0},{3,1},{4,6},{5,7},{6,4},{7,5},{8,10},{9,11},{10,... | collective-permute-start | bytes 196616 | tf_op jit(solution)/shard_map/ppermute | solution.py:266
  107.4 3.8 %collective-permute-start.7 = (f32[4,8,512]{2,1,0:T(8,128)S(1)}, f32[4,8,512]{2,1,0:T(8,128)S(1)}, u32[]{:S(2)}, u32[]{:S(2)}) collective-permute-start(f32[4,8,512]{2,1,0:T(8,128)S(1)} %get-tuple-element.108), channel_id=1, source_target_pairs={{0,3},{1,0},{2,1},{3,2},{4,7},{5,4},{6,5},{7,6},{8,11},{9,8},{10,9... | collective-permute-start | bytes 196616 | tf_op jit(solution)/shard_map/ppermute | solution.py:266

commit v6 on v5

--- a/solution.py
+++ b/solution.py
@@ -274,34 +274,50 @@
     return jnp.concatenate(pieces, axis)
 
 
-def field_halos(fields, y_prev, y_next, z_prev, z_next):
+def field_halos(fields, y_prev, y_next, z_prev, z_next, corner_pp, corner_np):
     rows = lax.axis_size("row")
     cols = lax.axis_size("col")
+    both = ("row", "col")
+
+    def flat(r, c):
+        return r * cols + c
+
     down_rows = [(i, i + 1) for i in range(rows - 1)]
     up_rows = [(i + 1, i) for i in range(rows - 1)]
     down_cols = [(i, i + 1) for i in range(cols - 1)]
     up_cols = [(i + 1, i) for i in range(cols - 1)]
+    diag_pp = [
+        (flat(r, c), flat(r + 1, c + 1)) for r in range(rows - 1) for c in range(cols - 1)
+    ]
+    diag_np = [
+        (flat(r + 1, c), flat(r, c + 1)) for r in range(rows - 1) for c in range(cols - 1)
+    ]
 
     def exchange(pieces_of, chosen, pairs, axis):
-        moved = lax.ppermute(jnp.stack([pieces_of[k] for k in chosen]), axis, pairs)
+        if not chosen:
+            return {}
+        moved = lax.ppermute(jnp.stack([pieces_of(k) for k in chosen]), axis, pairs)
         return {k: moved[n] for n, k in enumerate(chosen)}
 
-    from_prev = exchange([f[-1:] for f in fields], y_prev, down_rows, "row")
-    from_next = exchange([f[:1] for f in fields], y_next, up_rows, "row")
-    ext_y = []
+    got_yp = exchange(lambda k: fields[k][-1:], y_prev, down_rows, "row")
+    got_yn = exchange(lambda k: fields[k][:1], y_next, up_rows, "row")
+    got_zp = exchange(lambda k: fields[k][:, -1:], z_prev, down_cols, "col")
+    got_zn = exchange(lambda k: fields[k][:, :1], z_next, up_cols, "col")
+    got_pp = exchange(lambda k: fields[k][-1:, -1:], corner_pp, diag_pp, both)
+    got_np = exchange(lambda k: fields[k][:1, -1:], corner_np, diag_np, both)
+    ext = []
     for k, f in enumerate(fields):
-        zero = jnp.zeros_like(f[:1])
-        ext_y.append(
-            jnp.concatenate([from_prev.get(k, zero), f, from_next.get(k, zero)], 0)
+        row_zero = jnp.zeros_like(f[:1])
+        col_zero = jnp.zeros_like(f[:, :1])
+        cell_zero = jnp.zeros_like(f[:1, :1])
+        top = jnp.concatenate(
+            [got_pp.get(k, cell_zero), got_yp.get(k, row_zero), cell_zero], 1
         )
-    from_left = exchange([e[:, -1:] for e in ext_y], z_prev, down_cols, "col")
-    from_right = exchange([e[:, :1] for e in ext_y], z_next, up_cols, "col")
-    ext = []
-    for k, e in enumerate(ext_y):
-        zero = jnp.zeros_like(e[:, :1])
-        ext.append(
-            jnp.concatenate([from_left.get(k, zero), e, from_right.get(k, zero)], 1)
+        middle = jnp.concatenate([got_zp.get(k, col_zero), f, got_zn.get(k, col_zero)], 1)
+        bottom = jnp.concatenate(
+            [got_np.get(k, cell_zero), got_yn.get(k, row_zero), cell_zero], 1
         )
+        ext.append(jnp.concatenate([top, middle, bottom], 0))
     return ext
 
 
@@ -320,6 +336,8 @@
         y_next=(2,),
         z_prev=(0, 2, 3, 4, 6, 7),
         z_next=(0,),
+        corner_pp=(2, 3),
+        corner_np=(2,),
     )
     inside = inside_mask(count_y, count_z)
     ex_e, ey_e, ez_e = ext[0], ext[1], ext[2]

time: 117 us -> 132 us (1.13)
  starting transfers between devices: 47.9 us -> 57.4 us
  local copies, waits for them, and re-layouts: 12.7 us -> 18 us
    ppermute x4 -> x6, starting transfers between devices: 12.8 us -> 19 us  [exchange(): moved = lax.ppermute(jnp.stack([pieces_of(k) for k in chosen]), axis, pairs)]
    all_to_all x1, starting transfers between devices: 22.4 us -> 27 us  [on_device(): lax.all_to_all(payload, 'row', split_axis=0, concat_axis=0, tiled=True)]
    another operation x3 -> x8, local copies, waits for them, and re-layouts: 0.01 us -> 3.09 us  [the longest x6 3.08 us: exchange(): moved = lax.ppermute(jnp.stack([pieces_of(k) for k in chosen]), axis, pairs)]
    unnamed x39 -> x43, local copies, waits for them, and re-layouts: 6.77 us -> 8.87 us
    ppermute x6, starting transfers between devices: 8.17 us -> 6.81 us  [gather_cols(): lax.ppermute(block, 'col', [(i, (i + shift) % cols) for i in range(cols)])]
    ppermute x4 -> x6, waiting for transfers between devices: 2.79 us -> 2.07 us  [exchange(): moved = lax.ppermute(jnp.stack([pieces_of(k) for k in chosen]), axis, pairs)]
  transfers between devices with their start and end apart: 12 -> 14, of which waited for: 6 -> 6; matrix products, arithmetic and copies ran while one was open for 6% -> 10% of each run, Pallas kernels for 3% -> 3%
where the time goes in v6:
time: 132 us; the launch traced here: 131 us
  starting transfers between devices  57.4 us (43%)
  waiting for transfers between devices  29 us (22%)
  local copies, waits for them, and re-layouts  18 us (14%)
  other arithmetic  12.6 us (10%)
  Pallas kernels  12.2 us (9%)
  between operations  1.78 us (1%)
    all_to_all x1, starting transfers between devices, on_device(): lax.all_to_all(payload, 'row', split_axis=0, concat_axis=0, tiled=True)  27 us
    ppermute x6, starting transfers between devices, exchange(): moved = lax.ppermute(jnp.stack([pieces_of(k) for k in chosen]), axis, pairs)  19 us
    pallas_call x4, Pallas kernels, solve_lines(): pl.pallas_call(kernel, out_shape=jax.ShapeDtypeStruct(source.shape, sourc...  12.2 us
    all_to_all x1, waiting for transfers between devices, on_device(): lax.all_to_all(payload, 'row', split_axis=0, concat_axis=0, tiled=True)  12.2 us
    all_to_all x1, waiting for transfers between devices, on_device(): lax.all_to_all(answer, 'row', split_axis=0, concat_axis=0, tiled=True)  11 us
    unnamed x43, local copies, waits for them, and re-layouts  8.87 us
    ppermute x6, starting transfers between devices, gather_cols(): lax.ppermute(block, 'col', [(i, (i + shift) % cols) for i in range(cols)])  6.81 us
    all_to_all x1, starting transfers between devices, on_device(): lax.all_to_all(answer, 'row', split_axis=0, concat_axis=0, tiled=True)  4.6 us
  transfers between devices with their start and end apart: 14, of which 6 were waited for; matrix products, arithmetic and copies ran while one was open for 10% of the time, Pallas kernels for 3%

profile of v6, /device:TPU:1, one launch (start us, length us, event | category | flops | bytes accessed | tf_op | source)
XLA Modules:
  0.0 131.0 jit_solution(4634018612991700800)
XLA Ops:
  1.4 1.3 collective-permute-start.4
  3.5 6.6 %collective-permute-start.2 = (f32[2,1,1,512]{3,2,1,0:T(1,128)S(1)}, f32[2,1,1,512]{3,2,1,0:T(1,128)S(1)}, u32[]{:S(2)}, u32[]{:S(2)}) collective-permute-start(f32[2,1,1,512]{3,2,1,0:T(1,128)S(1)} %pad_maximum_fusion.30), channel_id=1, source_target_pairs={{0,5},{1,6},{2,7},{4,9},{5,10},{6,11},{8,13},{9,14},{10,15},{12,17... | collective-permute-start | bytes 12296 | tf_op jit(solution)/shard_map/ppermute | solution.py:299
  10.9 2.5 %collective-permute-start.3 = (f32[1,4,1,512]{3,2,1,0:T(1,128)S(1)}, f32[1,4,1,512]{3,2,1,0:T(1,128)S(1)}, u32[]{:S(2)}, u32[]{:S(2)}) collective-permute-start(f32[1,4,1,512]{3,2,1,0:T(1,128)S(1)} %slice_bitcast_fusion.17), channel_id=1, source_target_pairs={{1,0},{2,1},{3,2},{5,4},{6,5},{7,6},{9,8},{10,9},{11,10},{13,12},{... | collective-permute-start | bytes 24584 | tf_op jit(solution)/shard_map/ppermute | solution.py:299
  14.2 1.3 collective-permute-start.5
  19.0 3.0 %collective-permute-start.1 = (f32[6,4,1,512]{3,2,1,0:T(1,128)S(1)}, f32[6,4,1,512]{3,2,1,0:T(1,128)S(1)}, u32[]{:S(2)}, u32[]{:S(2)}) collective-permute-start(f32[6,4,1,512]{3,2,1,0:T(1,128)S(1)} %constant_dynamic-update-slice_fusion.6), channel_id=1, source_target_pairs={{0,1},{1,2},{2,3},{4,5},{5,6},{6,7},{8,9},{9,10},{10,11},{12,13},{... | collective-permute-start | bytes 147464 | tf_op jit(solution)/shard_map/ppermute | solution.py:299
  24.0 4.3 %collective-permute-start = (f32[6,1,8,512]{3,2,1,0:T(8,128)S(1)}, f32[6,1,8,512]{3,2,1,0:T(8,128)S(1)}, u32[]{:S(2)}, u32[]{:S(2)}) collective-permute-start(f32[6,1,8,512]{3,2,1,0:T(8,128)S(1)} %constant_dynamic-update-slice_fusion), channel_id=1, source_target_pairs={{0,4},{4,8},{8,12},{12,16},{16,20},{20,24},{24,28},{28,32},{32,36}... | collective-permute-start | bytes 294920 | tf_op jit(solution)/shard_map/ppermute | solution.py:299
  28.4 2.1 %collective-permute-done = f32[6,1,8,512]{3,2,1,0:T(8,128)S(1)} collective-permute-done((f32[6,1,8,512]{3,2,1,0:T(8,128)S(1)}, f32[6,1,8,512]{3,2,1,0:T(8,128)S(1)}, u32[]{:S(2)}, u32[]{:S(2)}) %collective-permute-start) | collective-permute-done | bytes 98336 | tf_op jit(solution)/shard_map/ppermute | solution.py:299
  33.1 1.0 collective-permute-start.7
  35.6 3.6 %shard_map.127 = f32[4,9,512]{2,1,0:T(8,128)} custom-call(f32[4,9,512]{2,1,0:T(8,128)} %fusion.22.source_ref, f32[4,9,512]{2,1,0:T(8,128)} %slice.880.coupling_ref), custom_call_target="tpu_custom_call" | custom-call | tf_op jit(solution)/shard_map/pallas_call | solution.py:134
  43.2 3.2 %shard_map.128 = f32[5,32,512]{2,1,0:T(8,128)} custom-call(f32[5,32,512]{2,1,0:T(8,128)} %get-tuple-element.56.source_ref, f32[5,32,512]{2,1,0:T(8,128)} %get-tuple-element.55.coupling_ref), custom_call_target="tpu_custom_call" | custom-call | tf_op jit(solution)/shard_map/pallas_call | solution.py:134
  46.4 1.1 broadcast_select_fusion
  48.3 1.0 reshape.187
  49.3 27.0 %all-to-all-start = ((f32[64,1,640]{2,1,0:T(1,128)}), f32[64,1,640]{2,1,0:T(1,128)S(1)}, u32[]{:S(2)}, u32[]{:S(2)}) async-start(f32[64,1,640]{2,1,0:T(1,128)} %reshape.187), calls=%async_computation | async-start | bytes 327680 | tf_op jit(solution)/shard_map/all_to_all | solution.py:422
  76.4 12.2 %all-to-all-done = f32[64,1,640]{2,1,0:T(1,128)S(1)} async-done(((f32[64,1,640]{2,1,0:T(1,128)}), f32[64,1,640]{2,1,0:T(1,128)S(1)}, u32[]{:S(2)}, u32[]{:S(2)}) %all-to-all-start) | async-done | bytes 163872 | tf_op jit(solution)/shard_map/all_to_all | solution.py:422
  89.1 1.0 reduce
  93.5 4.6 %all-to-all-start.1 = ((f32[64,1,448]{2,1,0:T(1,128)}), f32[64,1,448]{2,1,0:T(1,128)S(1)}, u32[]{:S(2)}, u32[]{:S(2)}) async-start(f32[64,1,448]{2,1,0:T(1,128)} %reshape.189), calls=%async_computation.1 | async-start | bytes 262144 | tf_op jit(solution)/shard_map/all_to_all | solution.py:426
  98.8 11.0 %all-to-all-done.1 = f32[64,1,448]{2,1,0:T(1,128)S(1)} async-done(((f32[64,1,448]{2,1,0:T(1,128)}), f32[64,1,448]{2,1,0:T(1,128)S(1)}, u32[]{:S(2)}, u32[]{:S(2)}) %all-to-all-start.1) | async-done | bytes 114720 | tf_op jit(solution)/shard_map/all_to_all | solution.py:426
  112.3 2.6 %shard_map.130 = f32[4,8,512]{2,1,0:T(8,128)} custom-call(f32[4,8,512]{2,1,0:T(8,128)} %fusion.41.source_ref, f32[4,8,512]{2,1,0:T(8,128)} %get-tuple-element.78.coupling_ref), custom_call_target="tpu_custom_call" | custom-call | tf_op jit(solution)/shard_map/pallas_call | solution.py:134
  114.9 1.0 slice.990
  116.7 3.8 %collective-permute-start.11 = (f32[4,8,512]{2,1,0:T(8,128)S(1)}, f32[4,8,512]{2,1,0:T(8,128)S(1)}, u32[]{:S(2)}, u32[]{:S(2)}) collective-permute-start(f32[4,8,512]{2,1,0:T(8,128)S(1)} %get-tuple-element.109), channel_id=1, source_target_pairs={{0,1},{1,2},{2,3},{3,0},{4,5},{5,6},{6,7},{7,4},{8,9},{9,10},{10,1... | collective-permute-start | bytes 196616 | tf_op jit(solution)/shard_map/ppermute | solution.py:266
  120.4 1.6 %collective-permute-start.10 = (f32[4,8,512]{2,1,0:T(8,128)S(1)}, f32[4,8,512]{2,1,0:T(8,128)S(1)}, u32[]{:S(2)}, u32[]{:S(2)}) collective-permute-start(f32[4,8,512]{2,1,0:T(8,128)S(1)} %get-tuple-element.109), channel_id=1, source_target_pairs={{0,2},{1,3},{2,0},{3,1},{4,6},{5,7},{6,4},{7,5},{8,10},{9,11},{10,... | collective-permute-start | bytes 196616 | tf_op jit(solution)/shard_map/ppermute | solution.py:266
  122.8 2.5 %collective-permute-done.10 = f32[4,8,512]{2,1,0:T(8,128)S(1)} collective-permute-done((f32[4,8,512]{2,1,0:T(8,128)S(1)}, f32[4,8,512]{2,1,0:T(8,128)S(1)}, u32[]{:S(2)}, u32[]{:S(2)}) %collective-permute-start.10) | collective-permute-done | bytes 65568 | tf_op jit(solution)/shard_map/ppermute | solution.py:266
  126.6 2.8 %shard_map.129 = f32[4,32,512]{2,1,0:T(8,128)} custom-call(f32[4,32,512]{2,1,0:T(8,128)} %pad_maximum_fusion.13.source_ref, f32[4,32,512]{2,1,0:T(8,128)} %slice_bitcast_fusion.2.coupling_ref), custom_call_target="tpu_custom_call" | custom-call | tf_op jit(solution)/shard_map/pallas_call | solution.py:134
  129.4 1.7 %fusion.39 = (f32[4,8,512]{2,1,0:T(8,128)}, f32[4,8,512]{2,1,0:T(8,128)}) fusion(s32[]{:T(128)S(6)} %add.295, f32[4,32,512]{2,1,0:T(8,128)} %shard_map.129, f32[4,9,512]{2,1,0:T(8,128)S(1)} %get-tuple-element.52, f32[4,9,512]{2,1,0:T(8,128)S(1)} %get-tuple-element.51, s32[]{:T(128)S(6)} %select_n.281), kind=kLoop, calls=%fused_computation.139 | loop fusion | flops 65536 | bytes 524296 | tf_op jit(solution)/shard_map/add | solution.py:463
  (199 shorter events, 26.6 us)
Async XLA Ops:
  0.6 14.8 %copy-start = (f32[4,8,512]{2,1,0:T(8,128)S(1)}, f32[4,8,512]{2,1,0:T(8,128)}, u32[]{:S(2)}) copy-start(f32[4,8,512]{2,1,0:T(8,128)} %param.8) | copy-start | bytes 196612
  1.4 31.1 %collective-permute-start.4 = (f32[1,1,1,512]{3,2,1,0:T(1,128)S(1)}, f32[1,1,1,512]{3,2,1,0:T(1,128)S(1)}, u32[]{:S(2)}, u32[]{:S(2)}) collective-permute-start(f32[1,1,1,512]{3,2,1,0:T(1,128)S(1)} %get-tuple-element.150), channel_id=1, source_target_pairs={{4,1},{5,2},{6,3},{8,5},{9,6},{10,7},{12,9},{13,10},{14,11},{16,13... | collective-permute-start | bytes 6152 | tf_op jit(solution)/shard_map/ppermute | solution.py:299
  3.4 15.6 %copy-start.6 = (f32[4,8,512]{2,1,0:T(8,128)S(1)}, f32[4,8,512]{2,1,0:T(8,128)}, u32[]{:S(2)}) copy-start(f32[4,8,512]{2,1,0:T(8,128)} %param.15) | copy-start | bytes 196612
  3.5 20.5 %collective-permute-start.2 = (f32[2,1,1,512]{3,2,1,0:T(1,128)S(1)}, f32[2,1,1,512]{3,2,1,0:T(1,128)S(1)}, u32[]{:S(2)}, u32[]{:S(2)}) collective-permute-start(f32[2,1,1,512]{3,2,1,0:T(1,128)S(1)} %pad_maximum_fusion.30), channel_id=1, source_target_pairs={{0,5},{1,6},{2,7},{4,9},{5,10},{6,11},{8,13},{9,14},{10,15},{12,17... | collective-permute-start | bytes 12296 | tf_op jit(solution)/shard_map/ppermute | solution.py:299
  10.9 17.4 %collective-permute-start.3 = (f32[1,4,1,512]{3,2,1,0:T(1,128)S(1)}, f32[1,4,1,512]{3,2,1,0:T(1,128)S(1)}, u32[]{:S(2)}, u32[]{:S(2)}) collective-permute-start(f32[1,4,1,512]{3,2,1,0:T(1,128)S(1)} %slice_bitcast_fusion.17), channel_id=1, source_target_pairs={{1,0},{2,1},{3,2},{5,4},{6,5},{7,6},{9,8},{10,9},{11,10},{13,12},{... | collective-permute-start | bytes 24584 | tf_op jit(solution)/shard_map/ppermute | solution.py:299
  14.2 18.3 %collective-permute-start.5 = (f32[1,1,8,512]{3,2,1,0:T(8,128)S(1)}, f32[1,1,8,512]{3,2,1,0:T(8,128)S(1)}, u32[]{:S(2)}, u32[]{:S(2)}) collective-permute-start(f32[1,1,8,512]{3,2,1,0:T(8,128)S(1)} %slice_bitcast_fusion.10), channel_id=1, source_target_pairs={{4,0},{8,4},{12,8},{16,12},{20,16},{24,20},{28,24},{32,28},{36,32}... | collective-permute-start | bytes 49160 | tf_op jit(solution)/shard_map/ppermute | solution.py:299
  16.3 6.7 %copy-start.3 = (f32[4,8,512]{2,1,0:T(8,128)S(1)}, f32[4,8,512]{2,1,0:T(8,128)}, u32[]{:S(2)}) copy-start(f32[4,8,512]{2,1,0:T(8,128)} %param.10) | copy-start | bytes 196612
  18.1 4.9 %copy-start.5 = (f32[4,8,512]{2,1,0:T(8,128)S(1)}, f32[4,8,512]{2,1,0:T(8,128)}, u32[]{:S(2)}) copy-start(f32[4,8,512]{2,1,0:T(8,128)} %param.11) | copy-start | bytes 196612
  19.0 9.2 %collective-permute-start.1 = (f32[6,4,1,512]{3,2,1,0:T(1,128)S(1)}, f32[6,4,1,512]{3,2,1,0:T(1,128)S(1)}, u32[]{:S(2)}, u32[]{:S(2)}) collective-permute-start(f32[6,4,1,512]{3,2,1,0:T(1,128)S(1)} %constant_dynamic-update-slice_fusion.6), channel_id=1, source_target_pairs={{0,1},{1,2},{2,3},{4,5},{5,6},{6,7},{8,9},{9,10},{10,11},{12,13},{... | collective-permute-start | bytes 147464 | tf_op jit(solution)/shard_map/ppermute | solution.py:299
  22.3 1.5 %copy-start.7 = (f32[4,8,512]{2,1,0:T(8,128)S(1)}, f32[4,8,512]{2,1,0:T(8,128)}, u32[]{:S(2)}) copy-start(f32[4,8,512]{2,1,0:T(8,128)} %param.14) | copy-start | bytes 196612
  23.9 4.4 %copy-start.2 = (f32[4,8,512]{2,1,0:T(8,128)S(1)}, f32[4,8,512]{2,1,0:T(8,128)}, u32[]{:S(2)}) copy-start(f32[4,8,512]{2,1,0:T(8,128)} %param.12) | copy-start | bytes 196612
  24.0 6.4 %collective-permute-start = (f32[6,1,8,512]{3,2,1,0:T(8,128)S(1)}, f32[6,1,8,512]{3,2,1,0:T(8,128)S(1)}, u32[]{:S(2)}, u32[]{:S(2)}) collective-permute-start(f32[6,1,8,512]{3,2,1,0:T(8,128)S(1)} %constant_dynamic-update-slice_fusion), channel_id=1, source_target_pairs={{0,4},{4,8},{8,12},{12,16},{16,20},{20,24},{24,28},{28,32},{32,36}... | collective-permute-start | bytes 294920 | tf_op jit(solution)/shard_map/ppermute | solution.py:299
  30.8 0.8 copy-start.8
  30.8 0.9 copy-start.9
  32.7 8.5 %collective-permute-start.8 = (f32[2,5,8,512]{3,2,1,0:T(8,128)S(1)}, f32[2,5,8,512]{3,2,1,0:T(8,128)S(1)}, u32[]{:S(2)}, u32[]{:S(2)}) collective-permute-start(f32[2,5,8,512]{3,2,1,0:T(8,128)S(1)} %pad_maximum_fusion.27), channel_id=1, source_target_pairs={{0,1},{1,2},{2,3},{3,0},{4,5},{5,6},{6,7},{7,4},{8,9},{9,10},{10,1... | collective-permute-start | bytes 491528 | tf_op jit(solution)/shard_map/ppermute | solution.py:266
  33.1 8.2 %collective-permute-start.7 = (f32[2,5,8,512]{3,2,1,0:T(8,128)S(1)}, f32[2,5,8,512]{3,2,1,0:T(8,128)S(1)}, u32[]{:S(2)}, u32[]{:S(2)}) collective-permute-start(f32[2,5,8,512]{3,2,1,0:T(8,128)S(1)} %pad_maximum_fusion.27), channel_id=1, source_target_pairs={{0,2},{1,3},{2,0},{3,1},{4,6},{5,7},{6,4},{7,5},{8,10},{9,11},{10,... | collective-permute-start | bytes 491528 | tf_op jit(solution)/shard_map/ppermute | solution.py:266
  34.1 8.0 %collective-permute-start.6 = (f32[2,5,8,512]{3,2,1,0:T(8,128)S(1)}, f32[2,5,8,512]{3,2,1,0:T(8,128)S(1)}, u32[]{:S(2)}, u32[]{:S(2)}) collective-permute-start(f32[2,5,8,512]{3,2,1,0:T(8,128)S(1)} %pad_maximum_fusion.27), channel_id=1, source_target_pairs={{0,3},{1,0},{2,1},{3,2},{4,7},{5,4},{6,5},{7,6},{8,11},{9,8},{10,9... | collective-permute-start | bytes 491528 | tf_op jit(solution)/shard_map/ppermute | solution.py:266
  40.2 0.9 copy-start.1
  49.3 39.3 %all-to-all-start = ((f32[64,1,640]{2,1,0:T(1,128)}), f32[64,1,640]{2,1,0:T(1,128)S(1)}, u32[]{:S(2)}, u32[]{:S(2)}) async-start(f32[64,1,640]{2,1,0:T(1,128)} %reshape.187), calls=%async_computation | async-start | bytes 327680 | tf_op jit(solution)/shard_map/all_to_all | solution.py:422
  93.5 16.3 %all-to-all-start.1 = ((f32[64,1,448]{2,1,0:T(1,128)}), f32[64,1,448]{2,1,0:T(1,128)S(1)}, u32[]{:S(2)}, u32[]{:S(2)}) async-start(f32[64,1,448]{2,1,0:T(1,128)} %reshape.189), calls=%async_computation.1 | async-start | bytes 262144 | tf_op jit(solution)/shard_map/all_to_all | solution.py:426
  114.9 1.0 copy-start.4
  116.7 6.2 %collective-permute-start.11 = (f32[4,8,512]{2,1,0:T(8,128)S(1)}, f32[4,8,512]{2,1,0:T(8,128)S(1)}, u32[]{:S(2)}, u32[]{:S(2)}) collective-permute-start(f32[4,8,512]{2,1,0:T(8,128)S(1)} %get-tuple-element.109), channel_id=1, source_target_pairs={{0,1},{1,2},{2,3},{3,0},{4,5},{5,6},{6,7},{7,4},{8,9},{9,10},{10,1... | collective-permute-start | bytes 196616 | tf_op jit(solution)/shard_map/ppermute | solution.py:266
  120.4 4.9 %collective-permute-start.10 = (f32[4,8,512]{2,1,0:T(8,128)S(1)}, f32[4,8,512]{2,1,0:T(8,128)S(1)}, u32[]{:S(2)}, u32[]{:S(2)}) collective-permute-start(f32[4,8,512]{2,1,0:T(8,128)S(1)} %get-tuple-element.109), channel_id=1, source_target_pairs={{0,2},{1,3},{2,0},{3,1},{4,6},{5,7},{6,4},{7,5},{8,10},{9,11},{10,... | collective-permute-start | bytes 196616 | tf_op jit(solution)/shard_map/ppermute | solution.py:266
  122.1 3.8 %collective-permute-start.9 = (f32[4,8,512]{2,1,0:T(8,128)S(1)}, f32[4,8,512]{2,1,0:T(8,128)S(1)}, u32[]{:S(2)}, u32[]{:S(2)}) collective-permute-start(f32[4,8,512]{2,1,0:T(8,128)S(1)} %get-tuple-element.109), channel_id=1, source_target_pairs={{0,3},{1,0},{2,1},{3,2},{4,7},{5,4},{6,5},{7,6},{8,11},{9,8},{10,9... | collective-permute-start | bytes 196616 | tf_op jit(solution)/shard_map/ppermute | solution.py:266
